TPU v7x, 32 devices: a whole 2x2x4 slice. The times are simulated.
32 devices in a mesh: groups: 2 (over y), dp: 4 (over z), tensor: 2 (over x), layer: 2 (over core).
Axes of the slice: x: 2, y: 2, z: 4, core: 2. Of those that a mesh axis runs over, the one named last changes fastest.
Arguments:
- hidden_in: bfloat16 [2, 8, 512, 14336], P('layer', ('groups', 'dp'), None, 'tensor'), parts along dimension 1, may hold values from -6 to 6
- out_grad: bfloat16 [2, 8, 512, 4096], P('layer', ('groups', 'dp'), 'tensor'), parts along dimension 1, may hold values from -6 to 6
- proj_in: bfloat16 [2, 14336, 64], P('layer', 'tensor'), may hold values from -0.046875 to 0.046875
- proj_out: bfloat16 [2, 4096, 64], P('layer'), may hold values from -0.09375 to 0.09375
- query_grads: bfloat16 [2, 1024, 4096], P('layer', 'dp', 'tensor'), may hold values from -1.5 to 1.5
- lengths: int32 [8], P(('groups', 'dp')), parts along dimension 0, may hold values from 128 to 512, as said below
- query_decision: int32 [1024], P('dp'), may hold values from 0 to 1023
Outputs:
- influence: float32 [8, 1024], P(('groups', 'dp')), parts along dimension 0
There are 2 independent parts, one for each index of `groups`. A program takes and returns all parts, laid end to end along the dimension named above; an argument that names none is the same for every part. Nothing has to cross between parts.
Inputs may be any that keep to these rules, and one draw needn't show every extreme that they name: `lengths`: in each part one transcript has all 512 tokens live and another has exactly 128.
All inputs are finite; a program needn't handle non-finite values.
Results may differ from a plain program's by a relative error of at most 0.004.
Values may be sent and summed in bfloat16 or wider, within the bound.
No kernel may reach another device: no remote copies, remote signals or barrier semaphores. Data moves between devices by JAX's collectives and lax.ppermute only.
A program may use at most 64 MiB of HBM per device.

v0:
```python
import jax
import jax.numpy as jnp
from jax import lax
from jax.sharding import PartitionSpec as P

DECISIONS = 1024


def decision_table(decisions):
    return (decisions[:, None] == jnp.arange(DECISIONS, dtype=jnp.int32)[None, :]).astype(
        jnp.float32
    )


def body(hidden_in, out_grad, proj_in, proj_out, query_grads, lengths, query_decision):
    hidden_rows = hidden_in[0]
    grad_rows = out_grad[0]
    side_hidden = proj_in[0]
    side_width = proj_out[0]
    query_rows = query_grads[0]
    ex_count = hidden_rows.shape[0]
    seq_shard = grad_rows.shape[1]
    first_pos = lax.axis_index("tensor") * seq_shard
    positions = first_pos + jnp.arange(seq_shard, dtype=jnp.int32)
    live_tokens = (positions[None, :] < lengths[:, None]).astype(jnp.float32)
    right = jnp.einsum("etd,dp->etp", grad_rows, side_width, preferred_element_type=jnp.float32)
    right = (right * live_tokens[:, :, None]).astype(jnp.bfloat16)
    left = jnp.einsum("etf,fp->etp", hidden_rows, side_hidden, preferred_element_type=jnp.float32)
    left_own = lax.psum_scatter(left, "tensor", scatter_dimension=1, tiled=True)
    partial_value = jnp.einsum(
        "etp,etq->epq", left_own, right.astype(jnp.float32), precision=lax.Precision.HIGHEST
    )
    partial_value = partial_value / lengths.astype(jnp.float32)[:, None, None]
    grad_part = lax.psum_scatter(partial_value, "tensor", scatter_dimension=1, tiled=True)
    grad_flat = grad_part.reshape(ex_count, -1).astype(jnp.bfloat16)
    block_rows = lax.all_gather(query_rows, "dp", axis=0, tiled=True)
    block_decisions = lax.all_gather(query_decision, "dp", axis=0, tiled=True)
    scores = jnp.einsum("ek,qk->eq", grad_flat, block_rows, preferred_element_type=jnp.float32)
    partial_dec = jnp.dot(scores, decision_table(block_decisions), precision=lax.Precision.HIGHEST)
    result = lax.psum(partial_dec, ("tensor", "layer"))
    return result


def solution(mesh):
    in_specs = (
        P("layer", ("groups", "dp"), None, "tensor"),
        P("layer", ("groups", "dp"), "tensor", None),
        P("layer", "tensor", None),
        P("layer", None, None),
        P("layer", "dp", "tensor"),
        P(("groups", "dp")),
        P("dp"),
    )
    out_specs = P(("groups", "dp"), None)
    return jax.shard_map(body, mesh=mesh, in_specs=in_specs, out_specs=out_specs, check_vma=False)
```

profile of v0, /device:TPU:0, one launch (start us, length us, event | category | flops | bytes accessed | tf_op | source)
XLA Modules:
  0.0 130.6 jit_solution(11717772726066423702)
XLA Ops:
  7.4 0.0 copy-start
  7.4 0.0 copy-start.2
  7.4 0.0 copy-start.1
  7.4 0.0 reduce-scatter.3.cloned.1.call-start
  7.4 6.4 %fusion.11 = f32[1,512,64]{1,2,0:T(8,128)} fusion(bf16[1,1,512,7168]{3,2,1,0:T(8,128)(2,1)} %param.7, bf16[1,7168,64]{1,2,0:T(8,128)(2,1)} %param.9), kind=kOutput, calls=%fused_computation.10 | convolution fusion | flops 469762048 | bytes 8388608 | tf_op jit(solution)/shard_map/etf,fp->etp/dot_general | solution.py:28
  13.8 0.0 reduce-scatter.3.cloned.1.call-update
  13.8 0.0 reduce-scatter.5.cloned.1.call-start
  14.5 0.0 copy-done
  14.5 0.0 copy-done.2
  14.6 0.7 fusion.14
  15.2 11.8 %reduce-scatter.3.cloned.1.call-done = f32[1,256,64]{1,2,0:T(8,128)} async-done(((f32[1,512,64]{1,2,0:T(8,128)}), f32[1,256,64]{1,2,0:T(8,128)}) %reduce-scatter.3.cloned.1.call-update) | async-done | bytes 65552 | tf_op jit(solution)/shard_map/reduce_scatter | solution.py:29
  27.1 1.6 %fusion.17 = f32[1,64,64]{2,1,0:T(8,128)} fusion(bf16[256,64]{1,0:T(8,128)(2,1)S(1)} %fusion.14, f32[1,256,64]{1,2,0:T(8,128)} %reduce-scatter.3.cloned.1.call-done, f32[]{:T(128)} %bitcast.7), kind=kOutput, calls=%fused_computation.13 | convolution fusion | flops 12587008 | bytes 114692 | tf_op jit(solution)/shard_map/etp,etq->epq/dot_general | solution.py:30
  28.7 0.0 reduce-scatter.5.cloned.1.call-update
  28.7 0.0 all-gather.4.cloned.1.call-start
  28.7 0.5 all-gather.4.cloned.1.call-update
  29.3 0.0 copy-done.1
  29.3 10.9 %all-gather.1 = s32[4,1,256]{2,1,0:T(1,128)S(1)} all-gather(s32[1,1,256]{2,1,0:T(1,128)S(1)} %bitcast.43), channel_id=1, replica_groups=mesh['groups'=2,'dp'=4,'tensor'=2,'layer'=2] {'dp'}, dimensions={0}, use_global_device_ids=true | all-gather | bytes 5120 | tf_op jit(solution)/shard_map/all_gather | solution.py:37
  40.2 0.0 reduce-scatter.5.cloned.1.call-done
  40.2 0.7 convert_element_type.30
  40.9 0.1 reshape.54
  41.0 70.4 %all-gather.4.cloned.1.call-done = bf16[1,1024,2048]{2,1,0:T(8,128)(2,1)} async-done(((bf16[1,256,2048]{2,1,0:T(8,128)(2,1)}), bf16[1,1024,2048]{2,1,0:T(8,128)(2,1)}) %all-gather.4.cloned.1.call-update) | async-done | bytes 4194320 | tf_op jit(solution)/shard_map/all_gather | solution.py:36
  111.4 3.4 %fusion.18 = f32[1024,1]{0,1:T(1,128)S(1)} fusion(bf16[2048,1]{0,1:T(2,128)(2,1)S(1)} %reshape.54, bf16[1,1024,2048]{2,1,0:T(8,128)(2,1)} %all-gather.4.cloned.1.call-done), kind=kOutput, calls=%fused_computation.14 | convolution fusion | flops 4194304 | bytes 4202496 | tf_op jit(solution)/shard_map/ek,qk->eq/dot_general | solution.py:38
  114.7 1.5 %fusion.4 = f32[1,1024]{1,0:T(1,128)S(1)} fusion(f32[1024,1]{0,1:T(1,128)S(1)} %fusion.18, s32[1024]{0:T(1024)S(1)} %bitcast.42), kind=kOutput, calls=%fused_computation.5 | convolution fusion | flops 13631488 | bytes 12288 | tf_op jit(solution)/shard_map/dot_general | solution.py:39
  116.2 7.0 %psum.7 = f32[1,1024]{1,0:T(1,128)} all-reduce(f32[1,1024]{1,0:T(1,128)S(1)} %fusion.4), channel_id=1, replica_groups=mesh['groups'=2,'dp'=4,'tensor'=2,'layer'=2] {'tensor','layer'}, use_global_device_ids=true, to_apply=%region_2.0 | all-reduce | flops 1024 | bytes 8192 | tf_op jit(solution)/shard_map/psum | solution.py:40
  (1 shorter events, 0.0 us)
Async XLA Ops:
  7.4 7.2 %copy-start = (bf16[1,1,256,4096]{3,2,1,0:T(8,128)(2,1)S(1)}, bf16[1,1,256,4096]{3,2,1,0:T(8,128)(2,1)}, u32[]{:S(2)}) copy-start(bf16[1,1,256,4096]{3,2,1,0:T(8,128)(2,1)} %param.8) | copy-start | bytes 6291460
  7.4 7.2 %copy-start.2 = (bf16[1,4096,64]{1,2,0:T(8,128)(2,1)S(1)}, bf16[1,4096,64]{1,2,0:T(8,128)(2,1)}, u32[]{:S(2)}) copy-start(bf16[1,4096,64]{1,2,0:T(8,128)(2,1)} %param.10) | copy-start | bytes 1572868
  7.4 21.9 %copy-start.1 = (s32[256]{0:T(256)S(1)}, s32[256]{0:T(256)}, u32[]{:S(2)}) copy-start(s32[256]{0:T(256)} %param.13) | copy-start | bytes 3076
  7.4 19.7 %reduce-scatter.3.cloned.1.call-start = ((), (), s32[]{:S(2)}) async-start(), calls=%async_computation.2 | async-start | bytes 196608 | tf_op jit(solution)/shard_map/reduce_scatter | solution.py:29
  13.8 26.4 %reduce-scatter.5.cloned.1.call-start = ((), (), s32[]{:S(2)}) async-start(), calls=%async_computation.3 | async-start | bytes 49152 | tf_op jit(solution)/shard_map/reduce_scatter | solution.py:34
  28.7 82.7 %all-gather.4.cloned.1.call-start = ((), (), s32[]{:S(2)}) async-start(), calls=%async_computation.4 | async-start | bytes 5242880 | tf_op jit(solution)/shard_map/all_gather | solution.py:36
Sparse Core Ops, SparseCore 0:
  13.9 13.0 reduce-scatter.2
  29.2 9.9 reduce-scatter.4
Sparse Core Ops, SparseCore 1:
  30.7 80.6 all-gather.3
where the time goes:
time: 131 us
  waiting for transfers between devices  82.7 us (63%)
  blocking collectives  17.9 us (14%)
  between operations  15.5 us (12%)
  matrix products  13.5 us (10%)
    all_gather x1, waiting for transfers between devices, body(): block_rows = lax.all_gather(query_rows, 'dp', axis=0, tiled=True)  70.4 us
    reduce_scatter x1, waiting for transfers between devices, body(): left_own = lax.psum_scatter(left, 'tensor', scatter_dimension=1, tiled=True)  11.8 us
    all_gather x1, blocking collectives, body(): block_decisions = lax.all_gather(query_decision, 'dp', axis=0, tiled=True)  10.9 us
    psum x1, blocking collectives, body(): result = lax.psum(partial_dec, ('tensor', 'layer'))  6.99 us
    dot_general x1, matrix products, body(): jnp.einsum('etf,fp->etp', hidden_rows, side_hidden, preferred_element_typ...  6.41 us
    dot_general x1, matrix products, body(): jnp.einsum('ek,qk->eq', grad_flat, block_rows, preferred_element_type=jnp...  3.37 us
  transfers between devices with their start and end apart: 3, of which 2 were waited for; matrix products, arithmetic and copies ran while one was open for 1% of the time, Pallas kernels for 0%

commit v1 on v0

v1 whole, which is shorter than its diff:
```python
import jax
import jax.numpy as jnp
from jax import lax
from jax.sharding import PartitionSpec as P

DECISIONS = 1024


def body(hidden_in, out_grad, proj_in, proj_out, query_grads, lengths, query_decision):
    hidden_rows = hidden_in[0, 0]
    grad_rows = out_grad[0, 0]
    side_hidden = proj_in[0]
    side_width = proj_out[0]
    query_rows = query_grads[0]
    length = lengths[0]
    seq_shard = grad_rows.shape[0]
    first_pos = lax.axis_index("tensor") * seq_shard
    positions = first_pos + jnp.arange(seq_shard, dtype=jnp.int32)
    live = (positions < length).astype(jnp.float32)
    right = jnp.dot(grad_rows, side_width, preferred_element_type=jnp.float32)
    right = (right * live[:, None]).astype(jnp.bfloat16)
    right_full = lax.all_gather(right, "tensor", axis=0, tiled=True)
    left = jnp.dot(hidden_rows, side_hidden, preferred_element_type=jnp.float32)
    partial = jnp.dot(
        left.T, right_full.astype(jnp.float32), precision=lax.Precision.HIGHEST
    )
    partial = partial / length.astype(jnp.float32)
    grad_part = lax.psum_scatter(partial, "tensor", scatter_dimension=0, tiled=True)
    grad_flat = grad_part.reshape(1, -1).astype(jnp.bfloat16)
    grads_all = lax.all_gather(grad_flat, "dp", axis=0, tiled=True)
    scores = jnp.dot(grads_all, query_rows.T, preferred_element_type=jnp.float32)
    table = (
        query_decision[:, None] == jnp.arange(DECISIONS, dtype=jnp.int32)[None, :]
    ).astype(jnp.float32)
    partial_dec = jnp.dot(scores, table, precision=lax.Precision.HIGHEST)
    total = lax.psum(partial_dec, ("dp", "tensor", "layer"))
    row = lax.dynamic_slice_in_dim(total, lax.axis_index("dp"), 1, axis=0)
    return row


def solution(mesh):
    in_specs = (
        P("layer", ("groups", "dp"), None, "tensor"),
        P("layer", ("groups", "dp"), "tensor", None),
        P("layer", "tensor", None),
        P("layer", None, None),
        P("layer", "dp", "tensor"),
        P(("groups", "dp")),
        P("dp"),
    )
    out_specs = P(("groups", "dp"), None)
    return jax.shard_map(body, mesh=mesh, in_specs=in_specs, out_specs=out_specs, check_vma=False)
```

time: 131 us -> 114 us (0.87)
  waiting for transfers between devices: 82.7 us -> 11.9 us
  blocking collectives: 17.9 us -> 76.3 us
  matrix products: 13.5 us -> 9.12 us
  local copies, waits for them, and re-layouts: 0.1 us -> 1.48 us
    all_gather x1 -> x0, waiting for transfers between devices: 70.4 us -> none  [body(): block_rows = lax.all_gather(query_rows, 'dp', axis=0, tiled=True)]
    psum x1, blocking collectives: 6.99 us -> 57.6 us  [body(): total = lax.psum(partial_dec, ('dp', 'tensor', 'layer'))]
    all_gather x1 -> x2, blocking collectives: 10.9 us -> 18.7 us  [the longest x1 13.2 us: body(): grads_all = lax.all_gather(grad_flat, 'dp', axis=0, tiled=True)]
    dot_general x5, matrix products: 13.5 us -> 9.12 us  [the longest x1 5.61 us: body(): left = jnp.dot(hidden_rows, side_hidden, preferred_element_type=jnp.float32)]
    reduce_scatter x2 -> x1, waiting for transfers between devices: 11.8 us -> 11.9 us  [body(): lax.psum_scatter(partial, 'tensor', scatter_dimension=0, tiled=True)]
  transfers between devices with their start and end apart: 3 -> 1, of which waited for: 2 -> 1; matrix products, arithmetic and copies ran while one was open for 1% -> 0% of each run, Pallas kernels for 0% -> 0%
where the time goes in v1:
time: 114 us
  blocking collectives  76.3 us (67%)
  between operations  14.2 us (12%)
  waiting for transfers between devices  11.9 us (10%)
  matrix products  9.12 us (8%)
  local copies, waits for them, and re-layouts  1.48 us (1%)
    psum x1, blocking collectives, body(): total = lax.psum(partial_dec, ('dp', 'tensor', 'layer'))  57.6 us
    all_gather x1, blocking collectives, body(): grads_all = lax.all_gather(grad_flat, 'dp', axis=0, tiled=True)  13.2 us
    reduce_scatter x1, waiting for transfers between devices, body(): lax.psum_scatter(partial, 'tensor', scatter_dimension=0, tiled=True)  11.9 us
    dot_general x1, matrix products, body(): left = jnp.dot(hidden_rows, side_hidden, preferred_element_type=jnp.float32)  5.61 us
    all_gather x1, blocking collectives, body(): right_full = lax.all_gather(right, 'tensor', axis=0, tiled=True)  5.51 us
  transfers between devices with their start and end apart: 1, of which 1 were waited for; matrix products, arithmetic and copies ran while one was open for 0% of the time, Pallas kernels for 0%

profile of v1, /device:TPU:0, one launch (start us, length us, event | category | flops | bytes accessed | tf_op | source)
XLA Modules:
  0.0 113.7 jit_solution(15606715019655168779)
XLA Ops:
  6.5 0.0 copy-start
  6.5 0.0 copy-start.1
  6.5 0.0 copy-start.2
  6.5 0.0 reduce-scatter.2.cloned.1.call-start
  7.4 0.8 copy-done
  8.1 1.8 %fusion.7 = bf16[256,64]{0,1:T(8,128)(2,1)S(1)} fusion(bf16[1,1,256,4096]{3,2,1,0:T(8,128)(2,1)S(1)} %copy-done, bf16[1,4096,64]{1,2,0:T(8,128)(2,1)} %param.10, f32[256]{0:T(256)S(1)} %compare_convert_fusion), kind=kOutput, calls=%fused_computation.5 | convolution fusion | flops 134250496 | bytes 2655232 | tf_op jit(solution)/shard_map/dot_general | solution.py:20
  9.9 5.5 %all_gather.6 = bf16[512,64]{0,1:T(8,128)(2,1)S(1)} all-gather(bf16[256,64]{0,1:T(8,128)(2,1)S(1)} %fusion.7), channel_id=1, replica_groups=mesh['groups'=2,'dp'=4,'tensor'=2,'layer'=2] {'tensor'}, dimensions={0}, use_global_device_ids=true | all-gather | bytes 98304 | tf_op jit(solution)/shard_map/all_gather | solution.py:22
  15.5 5.6 %fusion = f32[512,64]{0,1:T(8,128)S(1)} fusion(bf16[1,1,512,7168]{3,2,1,0:T(8,128)(2,1)} %param.7, bf16[1,7168,64]{1,2,0:T(8,128)(2,1)} %param.9), kind=kOutput, calls=%fused_computation | convolution fusion | flops 469762048 | bytes 8388608 | tf_op jit(solution)/shard_map/dot_general | solution.py:23
  21.1 0.8 convolution_divide_fusion
  21.9 0.0 reduce-scatter.2.cloned.1.call-update
  21.9 11.9 %reduce-scatter.2.cloned.1.call-done = f32[32,64]{1,0:T(8,128)} async-done(((f32[64,64]{1,0:T(8,128)}), f32[32,64]{1,0:T(8,128)}) %reduce-scatter.2.cloned.1.call-update) | async-done | bytes 8208 | tf_op jit(solution)/shard_map/reduce_scatter | solution.py:28
  33.8 0.7 convert_element_type.32
  34.5 0.1 reshape.21
  34.6 13.2 %all-gather = bf16[4,1,2048]{2,1,0:T(2,128)(2,1)S(1)} all-gather(bf16[1,1,2048]{2,1,0:T(2,128)(2,1)S(1)} %reshape.21), channel_id=1, replica_groups=mesh['groups'=2,'dp'=4,'tensor'=2,'layer'=2] {'dp'}, dimensions={0}, use_global_device_ids=true | all-gather | bytes 20480 | tf_op jit(solution)/shard_map/all_gather | solution.py:30
  47.8 0.0 copy-done.1
  47.8 0.4 fusion.10
  48.2 0.0 copy-done.2
  48.2 0.5 fusion.12
  48.7 57.6 %psum.7 = f32[4,1024]{1,0:T(4,128)S(1)} all-reduce(f32[4,1024]{1,0:T(4,128)S(1)} %fusion.12), channel_id=1, replica_groups=mesh['groups'=2,'dp'=4,'tensor'=2,'layer'=2] {'dp','tensor','layer'}, use_global_device_ids=true, to_apply=%region_1.0 | all-reduce | flops 4096 | bytes 32768 | tf_op jit(solution)/shard_map/psum | solution.py:36
  106.3 0.6 constant_dynamic-slice_fusion
  (1 shorter events, 0.0 us)
Async XLA Ops:
  6.5 1.6 %copy-start = (bf16[1,1,256,4096]{3,2,1,0:T(8,128)(2,1)S(1)}, bf16[1,1,256,4096]{3,2,1,0:T(8,128)(2,1)}, u32[]{:S(2)}) copy-start(bf16[1,1,256,4096]{3,2,1,0:T(8,128)(2,1)} %param.8) | copy-start | bytes 6291460
  6.5 41.2 %copy-start.1 = (bf16[1,256,2048]{2,1,0:T(8,128)(2,1)S(1)}, bf16[1,256,2048]{2,1,0:T(8,128)(2,1)}, u32[]{:S(2)}) copy-start(bf16[1,256,2048]{2,1,0:T(8,128)(2,1)} %param.11) | copy-start | bytes 3145732
  6.5 41.6 %copy-start.2 = (s32[256]{0:T(256)S(1)}, s32[256]{0:T(256)}, u32[]{:S(2)}) copy-start(s32[256]{0:T(256)} %param.13) | copy-start | bytes 3076
  6.5 27.3 %reduce-scatter.2.cloned.1.call-start = ((), (), s32[]{:S(2)}) async-start(), calls=%async_computation.1 | async-start | bytes 49152 | tf_op jit(solution)/shard_map/reduce_scatter | solution.py:28
Sparse Core Ops, SparseCore 0:
  22.0 11.7 reduce-scatter.1

commit v2 on v1

v2 whole, which is shorter than its diff:
```python
import jax
import jax.numpy as jnp
from jax import lax
from jax.sharding import PartitionSpec as P

DECISIONS = 1024


def shifted(x, axis, size, shift):
    return lax.ppermute(x, axis, [(i, (i + shift) % size) for i in range(size)])


def body(hidden_in, out_grad, proj_in, proj_out, query_grads, lengths, query_decision):
    tensors = lax.axis_size("tensor")
    dps = lax.axis_size("dp")
    layers = lax.axis_size("layer")
    me_t = lax.axis_index("tensor")
    me_d = lax.axis_index("dp")
    hidden_rows = hidden_in[0, 0]
    grad_rows = out_grad[0, 0]
    query_rows = query_grads[0]
    length = lengths[0]
    seq_shard = grad_rows.shape[0]

    positions = me_t * seq_shard + jnp.arange(seq_shard, dtype=jnp.int32)
    live = (positions < length).astype(jnp.float32)
    right = jnp.dot(grad_rows, proj_out[0], preferred_element_type=jnp.float32)
    right = (right * live[:, None]).astype(jnp.bfloat16)
    received = [right] + [shifted(right, "tensor", tensors, s) for s in range(1, tensors)]

    left = jnp.dot(hidden_rows, proj_in[0], preferred_element_type=jnp.float32)
    partial = None
    for s, part in enumerate(received):
        owner = (me_t - s) % tensors
        rows = lax.dynamic_slice_in_dim(left, owner * seq_shard, seq_shard, axis=0)
        term = jnp.dot(rows.T, part.astype(jnp.float32), precision=lax.Precision.HIGHEST)
        partial = term if partial is None else partial + term

    block_rows = partial.shape[0] // tensors
    grad_part = lax.dynamic_slice_in_dim(partial, me_t * block_rows, block_rows, axis=0)
    for s in range(1, tensors):
        dest = (me_t + s) % tensors
        piece = lax.dynamic_slice_in_dim(partial, dest * block_rows, block_rows, axis=0)
        grad_part = grad_part + shifted(piece, "tensor", tensors, s)
    grad_part = grad_part / length.astype(jnp.float32)
    grad_flat = grad_part.reshape(1, -1).astype(jnp.bfloat16)

    grads = [grad_flat] + [shifted(grad_flat, "dp", dps, s) for s in range(1, dps)]
    grads = jnp.concatenate(grads, axis=0)
    scores = jnp.dot(grads, query_rows.T, preferred_element_type=jnp.float32)
    table = (
        query_decision[:, None] == jnp.arange(DECISIONS, dtype=jnp.int32)[None, :]
    ).astype(jnp.float32)
    partial_dec = jnp.dot(scores, table, precision=lax.Precision.HIGHEST)

    total = partial_dec[0:1]
    for s in range(1, dps):
        total = total + shifted(partial_dec[s : s + 1], "dp", dps, -s)
    if tensors > 1:
        if tensors == 2:
            total = total + shifted(total, "tensor", tensors, 1)
        else:
            total = lax.psum(total, "tensor")
    if layers == 2:
        total = total + shifted(total, "layer", layers, 1)
    else:
        total = lax.psum(total, "layer")
    return total


def solution(mesh):
    in_specs = (
        P("layer", ("groups", "dp"), None, "tensor"),
        P("layer", ("groups", "dp"), "tensor", None),
        P("layer", "tensor", None),
        P("layer", None, None),
        P("layer", "dp", "tensor"),
        P(("groups", "dp")),
        P("dp"),
    )
    out_specs = P(("groups", "dp"), None)
    return jax.shard_map(body, mesh=mesh, in_specs=in_specs, out_specs=out_specs, check_vma=False)
```

time: 114 us -> 38.5 us (0.34)
  blocking collectives: 76.3 us -> 0 us
  between operations: 14.2 us -> 0.91 us
  starting transfers between devices: 0.01 us -> 11.5 us
  waiting for transfers between devices: 11.9 us -> 15.8 us
    psum x1 -> x0, blocking collectives: 57.6 us -> none  [body(): total = lax.psum(partial_dec, ('dp', 'tensor', 'layer'))]
    all_gather x2 -> x0, blocking collectives: 18.7 us -> none  [the longest x1 13.2 us: body(): grads_all = lax.all_gather(grad_flat, 'dp', axis=0, tiled=True)]
    ppermute x0 -> x10, waiting for transfers between devices: none -> 15.8 us  [shifted(): return lax.ppermute(x, axis, [(i, (i + shift) % size) for i in range(size)])]
    reduce_scatter x1 -> x0, waiting for transfers between devices: 11.9 us -> none  [body(): lax.psum_scatter(partial, 'tensor', scatter_dimension=0, tiled=True)]
    ppermute x0 -> x10, starting transfers between devices: none -> 11.5 us  [shifted(): return lax.ppermute(x, axis, [(i, (i + shift) % size) for i in range(size)])]
    dot_general x4 -> x5, matrix products: 8.61 us -> 8.14 us  [the longest x1 5.61 us: body(): left = jnp.dot(hidden_rows, proj_in[0], preferred_element_type=jnp.float32)]
  transfers between devices with their start and end apart: 1 -> 10, of which waited for: 1 -> 9; matrix products, arithmetic and copies ran while one was open for 0% -> 15% of each run, Pallas kernels for 0% -> 0%
where the time goes in v2:
time: 38.5 us; the launch traced here: 38.4 us
  waiting for transfers between devices  15.8 us (41%)
  starting transfers between devices  11.5 us (30%)
  matrix products  8.65 us (22%)
  local copies, waits for them, and re-layouts  0.91 us (2%)
  between operations  0.91 us (2%)
  other arithmetic  0.63 us (2%)
    ppermute x10, waiting for transfers between devices, shifted(): return lax.ppermute(x, axis, [(i, (i + shift) % size) for i in range(size)])  15.8 us
    ppermute x10, starting transfers between devices, shifted(): return lax.ppermute(x, axis, [(i, (i + shift) % size) for i in range(size)])  11.5 us
    dot_general x1, matrix products, body(): left = jnp.dot(hidden_rows, proj_in[0], preferred_element_type=jnp.float32)  5.61 us
    dot_general x1, matrix products, body(): right = jnp.dot(grad_rows, proj_out[0], preferred_element_type=jnp.float32)  1.8 us
    unnamed x6, local copies, waits for them, and re-layouts  0.8 us
  transfers between devices with their start and end apart: 10, of which 9 were waited for; matrix products, arithmetic and copies ran while one was open for 15% of the time, Pallas kernels for 0%

profile of v2, /device:TPU:0, one launch (start us, length us, event | category | flops | bytes accessed | tf_op | source)
XLA Modules:
  0.0 38.4 jit_solution(1916189448872213977)
XLA Ops:
  0.0 0.0 copy-start
  0.8 0.8 %copy-done = bf16[1,1,256,4096]{3,2,1,0:T(8,128)(2,1)S(1)} copy-done((bf16[1,1,256,4096]{3,2,1,0:T(8,128)(2,1)S(1)}, bf16[1,1,256,4096]{3,2,1,0:T(8,128)(2,1)}, u32[]{:S(2)}) %copy-start) | copy-done | bytes 2097176
  1.6 1.8 %fusion.7 = bf16[256,64]{0,1:T(8,128)(2,1)S(1)} fusion(bf16[1,1,256,4096]{3,2,1,0:T(8,128)(2,1)S(1)} %copy-done, bf16[1,4096,64]{1,2,0:T(8,128)(2,1)} %param.10, f32[256]{0:T(256)S(1)} %compare_convert_fusion), kind=kOutput, calls=%fused_computation.5 | convolution fusion | flops 134250496 | bytes 2655232 | tf_op jit(solution)/shard_map/dot_general | solution.py:27
  3.4 3.0 %collective-permute-start = (bf16[256,64]{0,1:T(8,128)(2,1)S(1)}, bf16[256,64]{0,1:T(8,128)(2,1)S(1)}, u32[]{:S(2)}, u32[]{:S(2)}) collective-permute-start(bf16[256,64]{0,1:T(8,128)(2,1)S(1)} %fusion.7), channel_id=1, source_target_pairs={{0,2},{2,0},{1,3},{3,1},{4,6},{6,4},{5,7},{7,5},{8,10},{10,8},{9,1... | collective-permute-start | bytes 98312 | tf_op jit(solution)/shard_map/ppermute | solution.py:10
  6.4 5.6 %fusion = f32[512,64]{0,1:T(8,128)S(1)} fusion(bf16[1,1,512,7168]{3,2,1,0:T(8,128)(2,1)} %param.7, bf16[1,7168,64]{1,2,0:T(8,128)(2,1)} %param.9), kind=kOutput, calls=%fused_computation | convolution fusion | flops 469762048 | bytes 8388608 | tf_op jit(solution)/shard_map/dot_general | solution.py:31
  12.0 0.2 fusion.17
  12.3 0.0 collective-permute-done
  12.3 0.2 convolution_add_fusion
  12.5 0.1 collective-permute-start.1
  12.6 3.7 %collective-permute-done.1 = f32[32,64]{1,0:T(8,128)S(1)} collective-permute-done((f32[32,64]{1,0:T(8,128)S(1)}, f32[32,64]{1,0:T(8,128)S(1)}, u32[]{:S(2)}, u32[]{:S(2)}) %collective-permute-start.1) | collective-permute-done | bytes 8224 | tf_op jit(solution)/shard_map/ppermute | solution.py:10
  16.3 0.1 convert_element_type.34
  16.4 3.6 %collective-permute-start.4 = (bf16[1,2048]{1,0:T(2,128)(2,1)S(1)}, bf16[1,2048]{1,0:T(2,128)(2,1)S(1)}, u32[]{:S(2)}, u32[]{:S(2)}) collective-permute-start(bf16[1,2048]{1,0:T(2,128)(2,1)S(1)} %convert_element_type.34), channel_id=1, source_target_pairs={{0,12},{4,0},{8,4},{12,8},{1,13},{5,1},{9,5},{13,9},{2,14},{6,2},{... | collective-permute-start | bytes 12296 | tf_op jit(solution)/shard_map/ppermute | solution.py:10
  20.0 0.0 collective-permute-start.3
  20.0 1.0 %collective-permute-start.2 = (bf16[1,2048]{1,0:T(2,128)(2,1)S(1)}, bf16[1,2048]{1,0:T(2,128)(2,1)S(1)}, u32[]{:S(2)}, u32[]{:S(2)}) collective-permute-start(bf16[1,2048]{1,0:T(2,128)(2,1)S(1)} %convert_element_type.34), channel_id=1, source_target_pairs={{0,4},{4,8},{8,12},{12,0},{1,5},{5,9},{9,13},{13,1},{2,6},{6,10},{... | collective-permute-start | bytes 12296 | tf_op jit(solution)/shard_map/ppermute | solution.py:10
  21.0 0.4 collective-permute-done.4
  21.4 3.2 %collective-permute-done.3 = bf16[1,2048]{1,0:T(2,128)(2,1)S(1)} collective-permute-done((bf16[1,2048]{1,0:T(2,128)(2,1)S(1)}, bf16[1,2048]{1,0:T(2,128)(2,1)S(1)}, u32[]{:S(2)}, u32[]{:S(2)}) %collective-permute-start.3) | collective-permute-done | bytes 4128 | tf_op jit(solution)/shard_map/ppermute | solution.py:10
  24.5 0.9 %collective-permute-done.2 = bf16[1,2048]{1,0:T(2,128)(2,1)S(1)} collective-permute-done((bf16[1,2048]{1,0:T(2,128)(2,1)S(1)}, bf16[1,2048]{1,0:T(2,128)(2,1)S(1)}, u32[]{:S(2)}, u32[]{:S(2)}) %collective-permute-start.2) | collective-permute-done | bytes 4128 | tf_op jit(solution)/shard_map/ppermute | solution.py:10
  25.4 0.0 copy-done.1
  25.4 0.4 fusion.10
  25.8 0.0 copy-done.2
  25.8 0.5 %fusion.12 = f32[4,1024]{1,0:T(4,128)S(1)} fusion(f32[4,256]{1,0:T(4,128)S(1)} %fusion.10, s32[256]{0:T(256)S(1)} %copy-done.2), kind=kOutput, calls=%fused_computation.10 | convolution fusion | flops 12845056 | bytes 21504 | tf_op jit(solution)/shard_map/dot_general | solution.py:54
  26.3 0.6 %collective-permute-start.5 = (f32[1,1024]{1,0:T(1,128)S(1)}, f32[1,1024]{1,0:T(1,128)S(1)}, u32[]{:S(2)}, u32[]{:S(2)}) collective-permute-start(f32[1,1024]{1,0:T(1,128)S(1)} %get-tuple-element.5), channel_id=1, source_target_pairs={{0,12},{4,0},{8,4},{12,8},{1,13},{5,1},{9,5},{13,9},{2,14},{6,2},{... | collective-permute-start | bytes 12296 | tf_op jit(solution)/shard_map/ppermute | solution.py:10
  27.0 1.5 %collective-permute-start.7 = (f32[1,1024]{1,0:T(1,128)S(1)}, f32[1,1024]{1,0:T(1,128)S(1)}, u32[]{:S(2)}, u32[]{:S(2)}) collective-permute-start(f32[1,1024]{1,0:T(1,128)S(1)} %get-tuple-element.6), channel_id=1, source_target_pairs={{0,4},{4,8},{8,12},{12,0},{1,5},{5,9},{9,13},{13,1},{2,6},{6,10},{... | collective-permute-start | bytes 12296 | tf_op jit(solution)/shard_map/ppermute | solution.py:10
  28.4 1.1 %collective-permute-start.6 = (f32[1,1024]{1,0:T(1,128)S(1)}, f32[1,1024]{1,0:T(1,128)S(1)}, u32[]{:S(2)}, u32[]{:S(2)}) collective-permute-start(f32[1,1024]{1,0:T(1,128)S(1)} %get-tuple-element.7), channel_id=1, source_target_pairs={{0,8},{4,12},{8,0},{12,4},{1,9},{5,13},{9,1},{13,5},{2,10},{6,14},... | collective-permute-start | bytes 12296 | tf_op jit(solution)/shard_map/ppermute | solution.py:10
  29.6 0.5 %collective-permute-done.5 = f32[1,1024]{1,0:T(1,128)S(1)} collective-permute-done((f32[1,1024]{1,0:T(1,128)S(1)}, f32[1,1024]{1,0:T(1,128)S(1)}, u32[]{:S(2)}, u32[]{:S(2)}) %collective-permute-start.5) | collective-permute-done | bytes 4128 | tf_op jit(solution)/shard_map/ppermute | solution.py:10
  30.0 2.4 %collective-permute-done.7 = f32[1,1024]{1,0:T(1,128)S(1)} collective-permute-done((f32[1,1024]{1,0:T(1,128)S(1)}, f32[1,1024]{1,0:T(1,128)S(1)}, u32[]{:S(2)}, u32[]{:S(2)}) %collective-permute-start.7) | collective-permute-done | bytes 4128 | tf_op jit(solution)/shard_map/ppermute | solution.py:10
  32.4 0.6 %collective-permute-done.6 = f32[1,1024]{1,0:T(1,128)S(1)} collective-permute-done((f32[1,1024]{1,0:T(1,128)S(1)}, f32[1,1024]{1,0:T(1,128)S(1)}, u32[]{:S(2)}, u32[]{:S(2)}) %collective-permute-start.6) | collective-permute-done | bytes 4128 | tf_op jit(solution)/shard_map/ppermute | solution.py:10
  32.9 0.6 %collective-permute-start.8 = (f32[1,1024]{1,0:T(1,128)S(1)}, f32[1,1024]{1,0:T(1,128)S(1)}, u32[]{:S(2)}, u32[]{:S(2)}) collective-permute-start(f32[1,1024]{1,0:T(1,128)S(1)} %fusion.27), channel_id=1, source_target_pairs={{0,2},{2,0},{1,3},{3,1},{4,6},{6,4},{5,7},{7,5},{8,10},{10,8},{9,1... | collective-permute-start | bytes 12296 | tf_op jit(solution)/shard_map/ppermute | solution.py:10
  33.6 3.1 %collective-permute-done.8 = f32[1,1024]{1,0:T(1,128)S(1)} collective-permute-done((f32[1,1024]{1,0:T(1,128)S(1)}, f32[1,1024]{1,0:T(1,128)S(1)}, u32[]{:S(2)}, u32[]{:S(2)}) %collective-permute-start.8) | collective-permute-done | bytes 4128 | tf_op jit(solution)/shard_map/ppermute | solution.py:10
  36.6 0.0 collective-permute-start.9
  36.6 1.2 %collective-permute-done.9 = f32[1,1024]{1,0:T(1,128)S(1)} collective-permute-done((f32[1,1024]{1,0:T(1,128)S(1)}, f32[1,1024]{1,0:T(1,128)S(1)}, u32[]{:S(2)}, u32[]{:S(2)}) %collective-permute-start.9) | collective-permute-done | bytes 4128 | tf_op jit(solution)/shard_map/ppermute | solution.py:10
  37.8 0.6 %add.73 = f32[1,1024]{1,0:T(1,128)} add(f32[1,1024]{1,0:T(1,128)S(1)} %add.72, f32[1,1024]{1,0:T(1,128)S(1)} %collective-permute-done.9) | non-fusion elementwise | flops 1024 | bytes 12288 | tf_op jit(solution)/shard_map/add | solution.py:65
  (8 shorter events, 0.1 us)
Async XLA Ops:
  0.0 1.6 %copy-start = (bf16[1,1,256,4096]{3,2,1,0:T(8,128)(2,1)S(1)}, bf16[1,1,256,4096]{3,2,1,0:T(8,128)(2,1)}, u32[]{:S(2)}) copy-start(bf16[1,1,256,4096]{3,2,1,0:T(8,128)(2,1)} %param.8) | copy-start | bytes 6291460
  0.0 25.4 %copy-start.1 = (bf16[1,256,2048]{2,1,0:T(8,128)(2,1)S(1)}, bf16[1,256,2048]{2,1,0:T(8,128)(2,1)}, u32[]{:S(2)}) copy-start(bf16[1,256,2048]{2,1,0:T(8,128)(2,1)} %param.11) | copy-start | bytes 3145732
  0.0 25.8 %copy-start.2 = (s32[256]{0:T(256)S(1)}, s32[256]{0:T(256)}, u32[]{:S(2)}) copy-start(s32[256]{0:T(256)} %param.13) | copy-start | bytes 3076
  3.4 8.9 %collective-permute-start = (bf16[256,64]{0,1:T(8,128)(2,1)S(1)}, bf16[256,64]{0,1:T(8,128)(2,1)S(1)}, u32[]{:S(2)}, u32[]{:S(2)}) collective-permute-start(bf16[256,64]{0,1:T(8,128)(2,1)S(1)} %fusion.7), channel_id=1, source_target_pairs={{0,2},{2,0},{1,3},{3,1},{4,6},{6,4},{5,7},{7,5},{8,10},{10,8},{9,1... | collective-permute-start | bytes 98312 | tf_op jit(solution)/shard_map/ppermute | solution.py:10
  12.5 3.8 %collective-permute-start.1 = (f32[32,64]{1,0:T(8,128)S(1)}, f32[32,64]{1,0:T(8,128)S(1)}, u32[]{:S(2)}, u32[]{:S(2)}) collective-permute-start(f32[32,64]{1,0:T(8,128)S(1)} %constant_dynamic-slice_fusion), channel_id=1, source_target_pairs={{0,2},{2,0},{1,3},{3,1},{4,6},{6,4},{5,7},{7,5},{8,10},{10,8},{9,1... | collective-permute-start | bytes 24584 | tf_op jit(solution)/shard_map/ppermute | solution.py:10
  16.4 5.0 %collective-permute-start.4 = (bf16[1,2048]{1,0:T(2,128)(2,1)S(1)}, bf16[1,2048]{1,0:T(2,128)(2,1)S(1)}, u32[]{:S(2)}, u32[]{:S(2)}) collective-permute-start(bf16[1,2048]{1,0:T(2,128)(2,1)S(1)} %convert_element_type.34), channel_id=1, source_target_pairs={{0,12},{4,0},{8,4},{12,8},{1,13},{5,1},{9,5},{13,9},{2,14},{6,2},{... | collective-permute-start | bytes 12296 | tf_op jit(solution)/shard_map/ppermute | solution.py:10
  20.0 4.5 %collective-permute-start.3 = (bf16[1,2048]{1,0:T(2,128)(2,1)S(1)}, bf16[1,2048]{1,0:T(2,128)(2,1)S(1)}, u32[]{:S(2)}, u32[]{:S(2)}) collective-permute-start(bf16[1,2048]{1,0:T(2,128)(2,1)S(1)} %convert_element_type.34), channel_id=1, source_target_pairs={{0,8},{4,12},{8,0},{12,4},{1,9},{5,13},{9,1},{13,5},{2,10},{6,14},... | collective-permute-start | bytes 12296 | tf_op jit(solution)/shard_map/ppermute | solution.py:10
  20.0 5.4 %collective-permute-start.2 = (bf16[1,2048]{1,0:T(2,128)(2,1)S(1)}, bf16[1,2048]{1,0:T(2,128)(2,1)S(1)}, u32[]{:S(2)}, u32[]{:S(2)}) collective-permute-start(bf16[1,2048]{1,0:T(2,128)(2,1)S(1)} %convert_element_type.34), channel_id=1, source_target_pairs={{0,4},{4,8},{8,12},{12,0},{1,5},{5,9},{9,13},{13,1},{2,6},{6,10},{... | collective-permute-start | bytes 12296 | tf_op jit(solution)/shard_map/ppermute | solution.py:10
  26.3 3.7 %collective-permute-start.5 = (f32[1,1024]{1,0:T(1,128)S(1)}, f32[1,1024]{1,0:T(1,128)S(1)}, u32[]{:S(2)}, u32[]{:S(2)}) collective-permute-start(f32[1,1024]{1,0:T(1,128)S(1)} %get-tuple-element.5), channel_id=1, source_target_pairs={{0,12},{4,0},{8,4},{12,8},{1,13},{5,1},{9,5},{13,9},{2,14},{6,2},{... | collective-permute-start | bytes 12296 | tf_op jit(solution)/shard_map/ppermute | solution.py:10
  27.0 5.4 %collective-permute-start.7 = (f32[1,1024]{1,0:T(1,128)S(1)}, f32[1,1024]{1,0:T(1,128)S(1)}, u32[]{:S(2)}, u32[]{:S(2)}) collective-permute-start(f32[1,1024]{1,0:T(1,128)S(1)} %get-tuple-element.6), channel_id=1, source_target_pairs={{0,4},{4,8},{8,12},{12,0},{1,5},{5,9},{9,13},{13,1},{2,6},{6,10},{... | collective-permute-start | bytes 12296 | tf_op jit(solution)/shard_map/ppermute | solution.py:10
  28.4 4.5 %collective-permute-start.6 = (f32[1,1024]{1,0:T(1,128)S(1)}, f32[1,1024]{1,0:T(1,128)S(1)}, u32[]{:S(2)}, u32[]{:S(2)}) collective-permute-start(f32[1,1024]{1,0:T(1,128)S(1)} %get-tuple-element.7), channel_id=1, source_target_pairs={{0,8},{4,12},{8,0},{12,4},{1,9},{5,13},{9,1},{13,5},{2,10},{6,14},... | collective-permute-start | bytes 12296 | tf_op jit(solution)/shard_map/ppermute | solution.py:10
  32.9 3.7 %collective-permute-start.8 = (f32[1,1024]{1,0:T(1,128)S(1)}, f32[1,1024]{1,0:T(1,128)S(1)}, u32[]{:S(2)}, u32[]{:S(2)}) collective-permute-start(f32[1,1024]{1,0:T(1,128)S(1)} %fusion.27), channel_id=1, source_target_pairs={{0,2},{2,0},{1,3},{3,1},{4,6},{6,4},{5,7},{7,5},{8,10},{10,8},{9,1... | collective-permute-start | bytes 12296 | tf_op jit(solution)/shard_map/ppermute | solution.py:10
  36.6 1.2 %collective-permute-start.9 = (f32[1,1024]{1,0:T(1,128)S(1)}, f32[1,1024]{1,0:T(1,128)S(1)}, u32[]{:S(2)}, u32[]{:S(2)}) collective-permute-start(f32[1,1024]{1,0:T(1,128)S(1)} %add.72), channel_id=1, source_target_pairs={{0,1},{1,0},{2,3},{3,2},{4,5},{5,4},{6,7},{7,6},{8,9},{9,8},{10,11... | collective-permute-start | bytes 12296 | tf_op jit(solution)/shard_map/ppermute | solution.py:10

commit v3 on v2

--- a/solution.py
+++ b/solution.py
@@ -18,7 +18,8 @@
     me_d = lax.axis_index("dp")
     hidden_rows = hidden_in[0, 0]
     grad_rows = out_grad[0, 0]
-    query_rows = query_grads[0]
+    query_own = query_grads[0]
+    query_parts = [query_own] + [shifted(query_own, "tensor", tensors, s) for s in range(1, tensors)]
     length = lengths[0]
     seq_shard = grad_rows.shape[0]
 
@@ -36,18 +37,21 @@
         term = jnp.dot(rows.T, part.astype(jnp.float32), precision=lax.Precision.HIGHEST)
         partial = term if partial is None else partial + term
 
-    block_rows = partial.shape[0] // tensors
-    grad_part = lax.dynamic_slice_in_dim(partial, me_t * block_rows, block_rows, axis=0)
+    total_grad = partial
     for s in range(1, tensors):
-        dest = (me_t + s) % tensors
-        piece = lax.dynamic_slice_in_dim(partial, dest * block_rows, block_rows, axis=0)
-        grad_part = grad_part + shifted(piece, "tensor", tensors, s)
-    grad_part = grad_part / length.astype(jnp.float32)
-    grad_flat = grad_part.reshape(1, -1).astype(jnp.bfloat16)
+        total_grad = total_grad + shifted(partial, "tensor", tensors, s)
+    total_grad = total_grad / length.astype(jnp.float32)
+    grad_flat = total_grad.reshape(1, -1).astype(jnp.bfloat16)
 
     grads = [grad_flat] + [shifted(grad_flat, "dp", dps, s) for s in range(1, dps)]
     grads = jnp.concatenate(grads, axis=0)
-    scores = jnp.dot(grads, query_rows.T, preferred_element_type=jnp.float32)
+    entry_block = query_own.shape[1]
+    scores = None
+    for s, part in enumerate(query_parts):
+        owner = (me_t - s) % tensors
+        cols = lax.dynamic_slice_in_dim(grads, owner * entry_block, entry_block, axis=1)
+        term = jnp.dot(cols, part.T, preferred_element_type=jnp.float32)
+        scores = term if scores is None else scores + term
     table = (
         query_decision[:, None] == jnp.arange(DECISIONS, dtype=jnp.int32)[None, :]
     ).astype(jnp.float32)
@@ -56,11 +60,6 @@
     total = partial_dec[0:1]
     for s in range(1, dps):
         total = total + shifted(partial_dec[s : s + 1], "dp", dps, -s)
-    if tensors > 1:
-        if tensors == 2:
-            total = total + shifted(total, "tensor", tensors, 1)
-        else:
-            total = lax.psum(total, "tensor")
     if layers == 2:
         total = total + shifted(total, "layer", layers, 1)
     else:

time: 38.5 us -> 52.5 us (1.36)
  waiting for transfers between devices: 15.8 us -> 26.5 us
  matrix products: 8.65 us -> 10.3 us
  starting transfers between devices: 11.5 us -> 13.1 us
    ppermute x10, waiting for transfers between devices: 15.8 us -> 26.5 us  [shifted(): return lax.ppermute(x, axis, [(i, (i + shift) % size) for i in range(size)])]
    dot_general x1 -> x2, matrix products: 0.38 us -> 1.99 us  [body(): term = jnp.dot(cols, part.T, preferred_element_type=jnp.float32)]
    ppermute x10, starting transfers between devices: 11.5 us -> 13.1 us  [shifted(): return lax.ppermute(x, axis, [(i, (i + shift) % size) for i in range(size)])]
  transfers between devices with their start and end apart: 10 -> 10, of which waited for: 9 -> 8; matrix products, arithmetic and copies ran while one was open for 15% -> 12% of each run, Pallas kernels for 0% -> 0%
where the time goes in v3:
time: 52.5 us; the launch traced here: 52.3 us
  waiting for transfers between devices  26.5 us (50%)
  starting transfers between devices  13.1 us (25%)
  matrix products  10.3 us (20%)
  between operations  0.91 us (2%)
  local copies, waits for them, and re-layouts  0.9 us (2%)
  other arithmetic  0.71 us (1%)
    ppermute x10, waiting for transfers between devices, shifted(): return lax.ppermute(x, axis, [(i, (i + shift) % size) for i in range(size)])  26.5 us
    ppermute x10, starting transfers between devices, shifted(): return lax.ppermute(x, axis, [(i, (i + shift) % size) for i in range(size)])  13.1 us
    dot_general x1, matrix products, body(): left = jnp.dot(hidden_rows, proj_in[0], preferred_element_type=jnp.float32)  5.61 us
    dot_general x2, matrix products, body(): term = jnp.dot(cols, part.T, preferred_element_type=jnp.float32)  1.99 us
    dot_general x1, matrix products, body(): right = jnp.dot(grad_rows, proj_out[0], preferred_element_type=jnp.float32)  1.8 us
  transfers between devices with their start and end apart: 10, of which 8 were waited for; matrix products, arithmetic and copies ran while one was open for 12% of the time, Pallas kernels for 0%

profile of v3, /device:TPU:0, one launch (start us, length us, event | category | flops | bytes accessed | tf_op | source)
XLA Modules:
  0.0 52.3 jit_solution(4258895734353567017)
XLA Ops:
  0.8 0.8 %copy-done = bf16[1,1,256,4096]{3,2,1,0:T(8,128)(2,1)S(1)} copy-done((bf16[1,1,256,4096]{3,2,1,0:T(8,128)(2,1)S(1)}, bf16[1,1,256,4096]{3,2,1,0:T(8,128)(2,1)}, u32[]{:S(2)}) %copy-start) | copy-done | bytes 2097176
  1.6 1.8 %fusion.7 = bf16[256,64]{0,1:T(8,128)(2,1)S(1)} fusion(bf16[1,1,256,4096]{3,2,1,0:T(8,128)(2,1)S(1)} %copy-done, bf16[1,4096,64]{1,2,0:T(8,128)(2,1)} %param.10, f32[256]{0:T(256)S(1)} %compare_convert_fusion), kind=kOutput, calls=%fused_computation.5 | convolution fusion | flops 134250496 | bytes 2655232 | tf_op jit(solution)/shard_map/dot_general | solution.py:28
  3.4 3.0 %collective-permute-start = (bf16[256,64]{0,1:T(8,128)(2,1)S(1)}, bf16[256,64]{0,1:T(8,128)(2,1)S(1)}, u32[]{:S(2)}, u32[]{:S(2)}) collective-permute-start(bf16[256,64]{0,1:T(8,128)(2,1)S(1)} %fusion.7), channel_id=1, source_target_pairs={{0,2},{2,0},{1,3},{3,1},{4,6},{6,4},{5,7},{7,5},{8,10},{10,8},{9,1... | collective-permute-start | bytes 98312 | tf_op jit(solution)/shard_map/ppermute | solution.py:10
  6.4 0.1 collective-permute-start.5
  6.5 5.6 %fusion = f32[512,64]{0,1:T(8,128)S(1)} fusion(bf16[1,1,512,7168]{3,2,1,0:T(8,128)(2,1)} %param.7, bf16[1,7168,64]{1,2,0:T(8,128)(2,1)} %param.9), kind=kOutput, calls=%fused_computation | convolution fusion | flops 469762048 | bytes 8388608 | tf_op jit(solution)/shard_map/dot_general | solution.py:32
  12.1 0.2 fusion.15
  12.3 0.0 collective-permute-done
  12.3 0.2 convolution_add_fusion
  12.5 2.0 %collective-permute-start.1 = (f32[64,64]{1,0:T(8,128)S(1)}, f32[64,64]{1,0:T(8,128)S(1)}, u32[]{:S(2)}, u32[]{:S(2)}) collective-permute-start(f32[64,64]{1,0:T(8,128)S(1)} %convolution_add_fusion), channel_id=1, source_target_pairs={{0,2},{2,0},{1,3},{3,1},{4,6},{6,4},{5,7},{7,5},{8,10},{10,8},{9,1... | collective-permute-start | bytes 49160 | tf_op jit(solution)/shard_map/ppermute | solution.py:10
  14.5 17.4 %collective-permute-done.1 = f32[64,64]{1,0:T(8,128)S(1)} collective-permute-done((f32[64,64]{1,0:T(8,128)S(1)}, f32[64,64]{1,0:T(8,128)S(1)}, u32[]{:S(2)}, u32[]{:S(2)}) %collective-permute-start.1) | collective-permute-done | bytes 16416 | tf_op jit(solution)/shard_map/ppermute | solution.py:10
  32.0 0.1 convert_element_type.34
  32.1 3.7 %collective-permute-start.4 = (bf16[1,4096]{1,0:T(2,128)(2,1)S(1)}, bf16[1,4096]{1,0:T(2,128)(2,1)S(1)}, u32[]{:S(2)}, u32[]{:S(2)}) collective-permute-start(bf16[1,4096]{1,0:T(2,128)(2,1)S(1)} %convert_element_type.34), channel_id=1, source_target_pairs={{0,12},{4,0},{8,4},{12,8},{1,13},{5,1},{9,5},{13,9},{2,14},{6,2},{... | collective-permute-start | bytes 24584 | tf_op jit(solution)/shard_map/ppermute | solution.py:10
  35.7 0.0 collective-permute-start.3
  35.7 1.0 %collective-permute-start.2 = (bf16[1,4096]{1,0:T(2,128)(2,1)S(1)}, bf16[1,4096]{1,0:T(2,128)(2,1)S(1)}, u32[]{:S(2)}, u32[]{:S(2)}) collective-permute-start(bf16[1,4096]{1,0:T(2,128)(2,1)S(1)} %convert_element_type.34), channel_id=1, source_target_pairs={{0,4},{4,8},{8,12},{12,0},{1,5},{5,9},{9,13},{13,1},{2,6},{6,10},{... | collective-permute-start | bytes 24584 | tf_op jit(solution)/shard_map/ppermute | solution.py:10
  36.8 0.4 collective-permute-done.4
  37.2 3.2 %collective-permute-done.3 = bf16[1,4096]{1,0:T(2,128)(2,1)S(1)} collective-permute-done((bf16[1,4096]{1,0:T(2,128)(2,1)S(1)}, bf16[1,4096]{1,0:T(2,128)(2,1)S(1)}, u32[]{:S(2)}, u32[]{:S(2)}) %collective-permute-start.3) | collective-permute-done | bytes 8224 | tf_op jit(solution)/shard_map/ppermute | solution.py:10
  40.4 0.9 %collective-permute-done.2 = bf16[1,4096]{1,0:T(2,128)(2,1)S(1)} collective-permute-done((bf16[1,4096]{1,0:T(2,128)(2,1)S(1)}, bf16[1,4096]{1,0:T(2,128)(2,1)S(1)}, u32[]{:S(2)}, u32[]{:S(2)}) %collective-permute-start.2) | collective-permute-done | bytes 8224 | tf_op jit(solution)/shard_map/ppermute | solution.py:10
  41.3 0.1 pad_maximum_fusion
  41.4 0.0 collective-permute-done.5
  41.4 1.6 %fusion.17 = f32[4,256]{1,0:T(4,128)S(1)} fusion(bf16[256,2048]{1,0:T(8,128)(2,1)} %collective-permute-done.5, bf16[4,4096]{1,0:T(4,128)(2,1)S(1)} %pad_maximum_fusion, s32[]{:T(128)S(6)} %select_n.32), kind=kOutput, calls=%fused_computation.18 | convolution fusion | flops 4194304 | bytes 1069060 | tf_op jit(solution)/shard_map/dot_general | solution.py:53
  43.0 0.0 copy-done.1
  43.0 0.4 convolution_add_fusion.1
  43.4 0.5 fusion.10
  43.9 0.6 %collective-permute-start.6 = (f32[1,1024]{1,0:T(1,128)S(1)}, f32[1,1024]{1,0:T(1,128)S(1)}, u32[]{:S(2)}, u32[]{:S(2)}) collective-permute-start(f32[1,1024]{1,0:T(1,128)S(1)} %get-tuple-element.5), channel_id=1, source_target_pairs={{0,12},{4,0},{8,4},{12,8},{1,13},{5,1},{9,5},{13,9},{2,14},{6,2},{... | collective-permute-start | bytes 12296 | tf_op jit(solution)/shard_map/ppermute | solution.py:10
  44.5 1.5 %collective-permute-start.8 = (f32[1,1024]{1,0:T(1,128)S(1)}, f32[1,1024]{1,0:T(1,128)S(1)}, u32[]{:S(2)}, u32[]{:S(2)}) collective-permute-start(f32[1,1024]{1,0:T(1,128)S(1)} %get-tuple-element.6), channel_id=1, source_target_pairs={{0,4},{4,8},{8,12},{12,0},{1,5},{5,9},{9,13},{13,1},{2,6},{6,10},{... | collective-permute-start | bytes 12296 | tf_op jit(solution)/shard_map/ppermute | solution.py:10
  46.0 1.1 %collective-permute-start.7 = (f32[1,1024]{1,0:T(1,128)S(1)}, f32[1,1024]{1,0:T(1,128)S(1)}, u32[]{:S(2)}, u32[]{:S(2)}) collective-permute-start(f32[1,1024]{1,0:T(1,128)S(1)} %get-tuple-element.7), channel_id=1, source_target_pairs={{0,8},{4,12},{8,0},{12,4},{1,9},{5,13},{9,1},{13,5},{2,10},{6,14},... | collective-permute-start | bytes 12296 | tf_op jit(solution)/shard_map/ppermute | solution.py:10
  47.1 0.5 collective-permute-done.6
  47.6 2.4 %collective-permute-done.8 = f32[1,1024]{1,0:T(1,128)S(1)} collective-permute-done((f32[1,1024]{1,0:T(1,128)S(1)}, f32[1,1024]{1,0:T(1,128)S(1)}, u32[]{:S(2)}, u32[]{:S(2)}) %collective-permute-start.8) | collective-permute-done | bytes 4128 | tf_op jit(solution)/shard_map/ppermute | solution.py:10
  49.9 0.6 %collective-permute-done.7 = f32[1,1024]{1,0:T(1,128)S(1)} collective-permute-done((f32[1,1024]{1,0:T(1,128)S(1)}, f32[1,1024]{1,0:T(1,128)S(1)}, u32[]{:S(2)}, u32[]{:S(2)}) %collective-permute-start.7) | collective-permute-done | bytes 4128 | tf_op jit(solution)/shard_map/ppermute | solution.py:10
  50.5 0.1 collective-permute-start.9
  50.6 1.2 %collective-permute-done.9 = f32[1,1024]{1,0:T(1,128)S(1)} collective-permute-done((f32[1,1024]{1,0:T(1,128)S(1)}, f32[1,1024]{1,0:T(1,128)S(1)}, u32[]{:S(2)}, u32[]{:S(2)}) %collective-permute-start.9) | collective-permute-done | bytes 4128 | tf_op jit(solution)/shard_map/ppermute | solution.py:10
  51.7 0.6 %add.67 = f32[1,1024]{1,0:T(1,128)} add(f32[1,1024]{1,0:T(1,128)S(1)} %fusion.21, f32[1,1024]{1,0:T(1,128)S(1)} %collective-permute-done.9) | non-fusion elementwise | flops 1024 | bytes 12288 | tf_op jit(solution)/shard_map/add | solution.py:64
  (8 shorter events, 0.0 us)
Async XLA Ops:
  0.0 1.6 %copy-start = (bf16[1,1,256,4096]{3,2,1,0:T(8,128)(2,1)S(1)}, bf16[1,1,256,4096]{3,2,1,0:T(8,128)(2,1)}, u32[]{:S(2)}) copy-start(bf16[1,1,256,4096]{3,2,1,0:T(8,128)(2,1)} %param.8) | copy-start | bytes 6291460
  0.0 43.0 %copy-start.1 = (bf16[1,256,2048]{2,1,0:T(8,128)(2,1)S(1)}, bf16[1,256,2048]{2,1,0:T(8,128)(2,1)}, u32[]{:S(2)}) copy-start(bf16[1,256,2048]{2,1,0:T(8,128)(2,1)} %param.11) | copy-start | bytes 3145732
  0.0 43.4 %copy-start.2 = (s32[256]{0:T(256)S(1)}, s32[256]{0:T(256)}, u32[]{:S(2)}) copy-start(s32[256]{0:T(256)} %param.13) | copy-start | bytes 3076
  3.4 8.9 %collective-permute-start = (bf16[256,64]{0,1:T(8,128)(2,1)S(1)}, bf16[256,64]{0,1:T(8,128)(2,1)S(1)}, u32[]{:S(2)}, u32[]{:S(2)}) collective-permute-start(bf16[256,64]{0,1:T(8,128)(2,1)S(1)} %fusion.7), channel_id=1, source_target_pairs={{0,2},{2,0},{1,3},{3,1},{4,6},{6,4},{5,7},{7,5},{8,10},{10,8},{9,1... | collective-permute-start | bytes 98312 | tf_op jit(solution)/shard_map/ppermute | solution.py:10
  6.4 34.9 %collective-permute-start.5 = (bf16[256,2048]{1,0:T(8,128)(2,1)}, bf16[256,2048]{1,0:T(8,128)(2,1)}, u32[]{:S(2)}, u32[]{:S(2)}) collective-permute-start(bf16[256,2048]{1,0:T(8,128)(2,1)} %bitcast.26), channel_id=1, source_target_pairs={{0,2},{2,0},{1,3},{3,1},{4,6},{6,4},{5,7},{7,5},{8,10},{10,8},{9,1... | collective-permute-start | bytes 3145736 | tf_op jit(solution)/shard_map/ppermute | solution.py:10
  12.5 19.4 %collective-permute-start.1 = (f32[64,64]{1,0:T(8,128)S(1)}, f32[64,64]{1,0:T(8,128)S(1)}, u32[]{:S(2)}, u32[]{:S(2)}) collective-permute-start(f32[64,64]{1,0:T(8,128)S(1)} %convolution_add_fusion), channel_id=1, source_target_pairs={{0,2},{2,0},{1,3},{3,1},{4,6},{6,4},{5,7},{7,5},{8,10},{10,8},{9,1... | collective-permute-start | bytes 49160 | tf_op jit(solution)/shard_map/ppermute | solution.py:10
  32.1 5.1 %collective-permute-start.4 = (bf16[1,4096]{1,0:T(2,128)(2,1)S(1)}, bf16[1,4096]{1,0:T(2,128)(2,1)S(1)}, u32[]{:S(2)}, u32[]{:S(2)}) collective-permute-start(bf16[1,4096]{1,0:T(2,128)(2,1)S(1)} %convert_element_type.34), channel_id=1, source_target_pairs={{0,12},{4,0},{8,4},{12,8},{1,13},{5,1},{9,5},{13,9},{2,14},{6,2},{... | collective-permute-start | bytes 24584 | tf_op jit(solution)/shard_map/ppermute | solution.py:10
  35.7 4.6 %collective-permute-start.3 = (bf16[1,4096]{1,0:T(2,128)(2,1)S(1)}, bf16[1,4096]{1,0:T(2,128)(2,1)S(1)}, u32[]{:S(2)}, u32[]{:S(2)}) collective-permute-start(bf16[1,4096]{1,0:T(2,128)(2,1)S(1)} %convert_element_type.34), channel_id=1, source_target_pairs={{0,8},{4,12},{8,0},{12,4},{1,9},{5,13},{9,1},{13,5},{2,10},{6,14},... | collective-permute-start | bytes 24584 | tf_op jit(solution)/shard_map/ppermute | solution.py:10
  35.7 5.5 %collective-permute-start.2 = (bf16[1,4096]{1,0:T(2,128)(2,1)S(1)}, bf16[1,4096]{1,0:T(2,128)(2,1)S(1)}, u32[]{:S(2)}, u32[]{:S(2)}) collective-permute-start(bf16[1,4096]{1,0:T(2,128)(2,1)S(1)} %convert_element_type.34), channel_id=1, source_target_pairs={{0,4},{4,8},{8,12},{12,0},{1,5},{5,9},{9,13},{13,1},{2,6},{6,10},{... | collective-permute-start | bytes 24584 | tf_op jit(solution)/shard_map/ppermute | solution.py:10
  43.9 3.7 %collective-permute-start.6 = (f32[1,1024]{1,0:T(1,128)S(1)}, f32[1,1024]{1,0:T(1,128)S(1)}, u32[]{:S(2)}, u32[]{:S(2)}) collective-permute-start(f32[1,1024]{1,0:T(1,128)S(1)} %get-tuple-element.5), channel_id=1, source_target_pairs={{0,12},{4,0},{8,4},{12,8},{1,13},{5,1},{9,5},{13,9},{2,14},{6,2},{... | collective-permute-start | bytes 12296 | tf_op jit(solution)/shard_map/ppermute | solution.py:10
  44.5 5.4 %collective-permute-start.8 = (f32[1,1024]{1,0:T(1,128)S(1)}, f32[1,1024]{1,0:T(1,128)S(1)}, u32[]{:S(2)}, u32[]{:S(2)}) collective-permute-start(f32[1,1024]{1,0:T(1,128)S(1)} %get-tuple-element.6), channel_id=1, source_target_pairs={{0,4},{4,8},{8,12},{12,0},{1,5},{5,9},{9,13},{13,1},{2,6},{6,10},{... | collective-permute-start | bytes 12296 | tf_op jit(solution)/shard_map/ppermute | solution.py:10
  46.0 4.5 %collective-permute-start.7 = (f32[1,1024]{1,0:T(1,128)S(1)}, f32[1,1024]{1,0:T(1,128)S(1)}, u32[]{:S(2)}, u32[]{:S(2)}) collective-permute-start(f32[1,1024]{1,0:T(1,128)S(1)} %get-tuple-element.7), channel_id=1, source_target_pairs={{0,8},{4,12},{8,0},{12,4},{1,9},{5,13},{9,1},{13,5},{2,10},{6,14},... | collective-permute-start | bytes 12296 | tf_op jit(solution)/shard_map/ppermute | solution.py:10
  50.5 1.2 %collective-permute-start.9 = (f32[1,1024]{1,0:T(1,128)S(1)}, f32[1,1024]{1,0:T(1,128)S(1)}, u32[]{:S(2)}, u32[]{:S(2)}) collective-permute-start(f32[1,1024]{1,0:T(1,128)S(1)} %fusion.21), channel_id=1, source_target_pairs={{0,1},{1,0},{2,3},{3,2},{4,5},{5,4},{6,7},{7,6},{8,9},{9,8},{10,11... | collective-permute-start | bytes 12296 | tf_op jit(solution)/shard_map/ppermute | solution.py:10

commit v4 on v2

--- a/solution.py
+++ b/solution.py
@@ -15,7 +15,6 @@
     dps = lax.axis_size("dp")
     layers = lax.axis_size("layer")
     me_t = lax.axis_index("tensor")
-    me_d = lax.axis_index("dp")
     hidden_rows = hidden_in[0, 0]
     grad_rows = out_grad[0, 0]
     query_rows = query_grads[0]
@@ -56,15 +55,13 @@
     total = partial_dec[0:1]
     for s in range(1, dps):
         total = total + shifted(partial_dec[s : s + 1], "dp", dps, -s)
-    if tensors > 1:
-        if tensors == 2:
-            total = total + shifted(total, "tensor", tensors, 1)
-        else:
-            total = lax.psum(total, "tensor")
-    if layers == 2:
-        total = total + shifted(total, "layer", layers, 1)
+
+    peers = tensors * layers
+    if peers <= 4:
+        gathered = [shifted(total, ("tensor", "layer"), peers, s) for s in range(1, peers)]
+        total = total + sum(gathered)
     else:
-        total = lax.psum(total, "layer")
+        total = lax.psum(total, ("tensor", "layer"))
     return total
 
 

time: 38.5 us -> 37.4 us (0.971)
  waiting for transfers between devices: 15.8 us -> 14.5 us
    ppermute x10 -> x11, waiting for transfers between devices: 15.8 us -> 14.5 us  [shifted(): return lax.ppermute(x, axis, [(i, (i + shift) % size) for i in range(size)])]
    ppermute x10 -> x11, starting transfers between devices: 11.5 us -> 11.8 us  [shifted(): return lax.ppermute(x, axis, [(i, (i + shift) % size) for i in range(size)])]
  transfers between devices with their start and end apart: 10 -> 11, of which waited for: 9 -> 9; matrix products, arithmetic and copies ran while one was open for 15% -> 16% of each run, Pallas kernels for 0% -> 0%
where the time goes in v4:
time: 37.4 us; the launch traced here: 37.3 us
  waiting for transfers between devices  14.5 us (39%)
  starting transfers between devices  11.8 us (32%)
  matrix products  8.65 us (23%)
  local copies, waits for them, and re-layouts  0.91 us (2%)
  between operations  0.91 us (2%)
  other arithmetic  0.62 us (2%)
    ppermute x11, waiting for transfers between devices, shifted(): return lax.ppermute(x, axis, [(i, (i + shift) % size) for i in range(size)])  14.5 us
    ppermute x11, starting transfers between devices, shifted(): return lax.ppermute(x, axis, [(i, (i + shift) % size) for i in range(size)])  11.8 us
    dot_general x1, matrix products, body(): left = jnp.dot(hidden_rows, proj_in[0], preferred_element_type=jnp.float32)  5.61 us
    dot_general x1, matrix products, body(): right = jnp.dot(grad_rows, proj_out[0], preferred_element_type=jnp.float32)  1.8 us
    unnamed x6, local copies, waits for them, and re-layouts  0.8 us
  transfers between devices with their start and end apart: 11, of which 9 were waited for; matrix products, arithmetic and copies ran while one was open for 16% of the time, Pallas kernels for 0%

profile of v4, /device:TPU:0, one launch (start us, length us, event | category | flops | bytes accessed | tf_op | source)
XLA Modules:
  0.0 37.3 jit_solution(3121487364688560229)
XLA Ops:
  0.0 0.0 copy-start
  0.8 0.8 %copy-done = bf16[1,1,256,4096]{3,2,1,0:T(8,128)(2,1)S(1)} copy-done((bf16[1,1,256,4096]{3,2,1,0:T(8,128)(2,1)S(1)}, bf16[1,1,256,4096]{3,2,1,0:T(8,128)(2,1)}, u32[]{:S(2)}) %copy-start) | copy-done | bytes 2097176
  1.6 1.8 %fusion.7 = bf16[256,64]{0,1:T(8,128)(2,1)S(1)} fusion(bf16[1,1,256,4096]{3,2,1,0:T(8,128)(2,1)S(1)} %copy-done, bf16[1,4096,64]{1,2,0:T(8,128)(2,1)} %param.10, f32[256]{0:T(256)S(1)} %compare_convert_fusion), kind=kOutput, calls=%fused_computation.5 | convolution fusion | flops 134250496 | bytes 2655232 | tf_op jit(solution)/shard_map/dot_general | solution.py:26
  3.4 3.0 %collective-permute-start = (bf16[256,64]{0,1:T(8,128)(2,1)S(1)}, bf16[256,64]{0,1:T(8,128)(2,1)S(1)}, u32[]{:S(2)}, u32[]{:S(2)}) collective-permute-start(bf16[256,64]{0,1:T(8,128)(2,1)S(1)} %fusion.7), channel_id=1, source_target_pairs={{0,2},{2,0},{1,3},{3,1},{4,6},{6,4},{5,7},{7,5},{8,10},{10,8},{9,1... | collective-permute-start | bytes 98312 | tf_op jit(solution)/shard_map/ppermute | solution.py:10
  6.4 5.6 %fusion = f32[512,64]{0,1:T(8,128)S(1)} fusion(bf16[1,1,512,7168]{3,2,1,0:T(8,128)(2,1)} %param.7, bf16[1,7168,64]{1,2,0:T(8,128)(2,1)} %param.9), kind=kOutput, calls=%fused_computation | convolution fusion | flops 469762048 | bytes 8388608 | tf_op jit(solution)/shard_map/dot_general | solution.py:30
  12.0 0.2 fusion.17
  12.3 0.0 collective-permute-done
  12.3 0.2 convolution_add_fusion
  12.5 0.1 collective-permute-start.1
  12.6 3.7 %collective-permute-done.1 = f32[32,64]{1,0:T(8,128)S(1)} collective-permute-done((f32[32,64]{1,0:T(8,128)S(1)}, f32[32,64]{1,0:T(8,128)S(1)}, u32[]{:S(2)}, u32[]{:S(2)}) %collective-permute-start.1) | collective-permute-done | bytes 8224 | tf_op jit(solution)/shard_map/ppermute | solution.py:10
  16.3 0.1 convert_element_type.34
  16.4 3.6 %collective-permute-start.4 = (bf16[1,2048]{1,0:T(2,128)(2,1)S(1)}, bf16[1,2048]{1,0:T(2,128)(2,1)S(1)}, u32[]{:S(2)}, u32[]{:S(2)}) collective-permute-start(bf16[1,2048]{1,0:T(2,128)(2,1)S(1)} %convert_element_type.34), channel_id=1, source_target_pairs={{0,12},{4,0},{8,4},{12,8},{1,13},{5,1},{9,5},{13,9},{2,14},{6,2},{... | collective-permute-start | bytes 12296 | tf_op jit(solution)/shard_map/ppermute | solution.py:10
  20.0 0.0 collective-permute-start.3
  20.0 1.0 %collective-permute-start.2 = (bf16[1,2048]{1,0:T(2,128)(2,1)S(1)}, bf16[1,2048]{1,0:T(2,128)(2,1)S(1)}, u32[]{:S(2)}, u32[]{:S(2)}) collective-permute-start(bf16[1,2048]{1,0:T(2,128)(2,1)S(1)} %convert_element_type.34), channel_id=1, source_target_pairs={{0,4},{4,8},{8,12},{12,0},{1,5},{5,9},{9,13},{13,1},{2,6},{6,10},{... | collective-permute-start | bytes 12296 | tf_op jit(solution)/shard_map/ppermute | solution.py:10
  21.0 0.4 collective-permute-done.4
  21.4 3.2 %collective-permute-done.3 = bf16[1,2048]{1,0:T(2,128)(2,1)S(1)} collective-permute-done((bf16[1,2048]{1,0:T(2,128)(2,1)S(1)}, bf16[1,2048]{1,0:T(2,128)(2,1)S(1)}, u32[]{:S(2)}, u32[]{:S(2)}) %collective-permute-start.3) | collective-permute-done | bytes 4128 | tf_op jit(solution)/shard_map/ppermute | solution.py:10
  24.5 0.9 %collective-permute-done.2 = bf16[1,2048]{1,0:T(2,128)(2,1)S(1)} collective-permute-done((bf16[1,2048]{1,0:T(2,128)(2,1)S(1)}, bf16[1,2048]{1,0:T(2,128)(2,1)S(1)}, u32[]{:S(2)}, u32[]{:S(2)}) %collective-permute-start.2) | collective-permute-done | bytes 4128 | tf_op jit(solution)/shard_map/ppermute | solution.py:10
  25.4 0.4 %fusion.10 = f32[4,256]{1,0:T(4,128)S(1)} fusion(bf16[1,256,2048]{2,1,0:T(8,128)(2,1)S(1)} %copy-done.1, bf16[1,2048]{1,0:T(2,128)(2,1)S(1)} %collective-permute-done.4, bf16[1,2048]{1,0:T(2,128)(2,1)S(1)} %collective-permute-done.3, bf16[1,2048]{1,0:T(2,128)(2,1)S(1)} %collective-permute-done.2, bf16[1,2048]{1,0:T(2,128)(2,1)S(1)} %convert_element_type.34), kind=kOutput, calls=%fused_computation.7 | convolution fusion | flops 4259840 | bytes 1069056 | tf_op jit(solution)/shard_map/dot_general | solution.py:49
  25.8 0.5 %fusion.12 = f32[4,1024]{1,0:T(4,128)S(1)} fusion(f32[4,256]{1,0:T(4,128)S(1)} %fusion.10, s32[256]{0:T(256)S(1)} %copy-done.2), kind=kOutput, calls=%fused_computation.10 | convolution fusion | flops 12845056 | bytes 21504 | tf_op jit(solution)/shard_map/dot_general | solution.py:53
  26.3 0.6 %collective-permute-start.5 = (f32[1,1024]{1,0:T(1,128)S(1)}, f32[1,1024]{1,0:T(1,128)S(1)}, u32[]{:S(2)}, u32[]{:S(2)}) collective-permute-start(f32[1,1024]{1,0:T(1,128)S(1)} %get-tuple-element.5), channel_id=1, source_target_pairs={{0,12},{4,0},{8,4},{12,8},{1,13},{5,1},{9,5},{13,9},{2,14},{6,2},{... | collective-permute-start | bytes 12296 | tf_op jit(solution)/shard_map/ppermute | solution.py:10
  27.0 1.5 %collective-permute-start.7 = (f32[1,1024]{1,0:T(1,128)S(1)}, f32[1,1024]{1,0:T(1,128)S(1)}, u32[]{:S(2)}, u32[]{:S(2)}) collective-permute-start(f32[1,1024]{1,0:T(1,128)S(1)} %get-tuple-element.6), channel_id=1, source_target_pairs={{0,4},{4,8},{8,12},{12,0},{1,5},{5,9},{9,13},{13,1},{2,6},{6,10},{... | collective-permute-start | bytes 12296 | tf_op jit(solution)/shard_map/ppermute | solution.py:10
  28.4 1.1 %collective-permute-start.6 = (f32[1,1024]{1,0:T(1,128)S(1)}, f32[1,1024]{1,0:T(1,128)S(1)}, u32[]{:S(2)}, u32[]{:S(2)}) collective-permute-start(f32[1,1024]{1,0:T(1,128)S(1)} %get-tuple-element.7), channel_id=1, source_target_pairs={{0,8},{4,12},{8,0},{12,4},{1,9},{5,13},{9,1},{13,5},{2,10},{6,14},... | collective-permute-start | bytes 12296 | tf_op jit(solution)/shard_map/ppermute | solution.py:10
  29.6 0.5 %collective-permute-done.5 = f32[1,1024]{1,0:T(1,128)S(1)} collective-permute-done((f32[1,1024]{1,0:T(1,128)S(1)}, f32[1,1024]{1,0:T(1,128)S(1)}, u32[]{:S(2)}, u32[]{:S(2)}) %collective-permute-start.5) | collective-permute-done | bytes 4128 | tf_op jit(solution)/shard_map/ppermute | solution.py:10
  30.0 2.4 %collective-permute-done.7 = f32[1,1024]{1,0:T(1,128)S(1)} collective-permute-done((f32[1,1024]{1,0:T(1,128)S(1)}, f32[1,1024]{1,0:T(1,128)S(1)}, u32[]{:S(2)}, u32[]{:S(2)}) %collective-permute-start.7) | collective-permute-done | bytes 4128 | tf_op jit(solution)/shard_map/ppermute | solution.py:10
  32.4 0.6 %collective-permute-done.6 = f32[1,1024]{1,0:T(1,128)S(1)} collective-permute-done((f32[1,1024]{1,0:T(1,128)S(1)}, f32[1,1024]{1,0:T(1,128)S(1)}, u32[]{:S(2)}, u32[]{:S(2)}) %collective-permute-start.6) | collective-permute-done | bytes 4128 | tf_op jit(solution)/shard_map/ppermute | solution.py:10
  32.9 0.1 collective-permute-start.10
  33.0 0.6 %collective-permute-start.9 = (f32[1,1024]{1,0:T(1,128)S(1)}, f32[1,1024]{1,0:T(1,128)S(1)}, u32[]{:S(2)}, u32[]{:S(2)}) collective-permute-start(f32[1,1024]{1,0:T(1,128)S(1)} %fusion.27), channel_id=1, source_target_pairs={{0,2},{1,3},{2,0},{3,1},{4,6},{5,7},{6,4},{7,5},{8,10},{9,11},{10,... | collective-permute-start | bytes 12296 | tf_op jit(solution)/shard_map/ppermute | solution.py:10
  33.6 0.2 collective-permute-start.8
  33.8 0.6 %collective-permute-done.10 = f32[1,1024]{1,0:T(1,128)S(1)} collective-permute-done((f32[1,1024]{1,0:T(1,128)S(1)}, f32[1,1024]{1,0:T(1,128)S(1)}, u32[]{:S(2)}, u32[]{:S(2)}) %collective-permute-start.10) | collective-permute-done | bytes 4128 | tf_op jit(solution)/shard_map/ppermute | solution.py:10
  34.3 2.4 %collective-permute-done.9 = f32[1,1024]{1,0:T(1,128)S(1)} collective-permute-done((f32[1,1024]{1,0:T(1,128)S(1)}, f32[1,1024]{1,0:T(1,128)S(1)}, u32[]{:S(2)}, u32[]{:S(2)}) %collective-permute-start.9) | collective-permute-done | bytes 4128 | tf_op jit(solution)/shard_map/ppermute | solution.py:10
  36.7 0.0 collective-permute-done.8
  36.7 0.6 %add_add_fusion = f32[1,1024]{1,0:T(1,128)} fusion(f32[1,1024]{1,0:T(1,128)S(1)} %fusion.27, f32[1,1024]{1,0:T(1,128)S(1)} %collective-permute-done.10, f32[1,1024]{1,0:T(1,128)S(1)} %collective-permute-done.8, f32[1,1024]{1,0:T(1,128)S(1)} %collective-permute-done.9), kind=kLoop, calls=%fused_computation.28 | loop fusion | flops 3072 | bytes 20480 | tf_op jit(solution)/shard_map/add | solution.py:62
  (9 shorter events, 0.1 us)
Async XLA Ops:
  0.0 1.6 %copy-start = (bf16[1,1,256,4096]{3,2,1,0:T(8,128)(2,1)S(1)}, bf16[1,1,256,4096]{3,2,1,0:T(8,128)(2,1)}, u32[]{:S(2)}) copy-start(bf16[1,1,256,4096]{3,2,1,0:T(8,128)(2,1)} %param.8) | copy-start | bytes 6291460
  0.0 25.4 %copy-start.1 = (bf16[1,256,2048]{2,1,0:T(8,128)(2,1)S(1)}, bf16[1,256,2048]{2,1,0:T(8,128)(2,1)}, u32[]{:S(2)}) copy-start(bf16[1,256,2048]{2,1,0:T(8,128)(2,1)} %param.11) | copy-start | bytes 3145732
  0.0 25.8 %copy-start.2 = (s32[256]{0:T(256)S(1)}, s32[256]{0:T(256)}, u32[]{:S(2)}) copy-start(s32[256]{0:T(256)} %param.13) | copy-start | bytes 3076
  3.4 8.9 %collective-permute-start = (bf16[256,64]{0,1:T(8,128)(2,1)S(1)}, bf16[256,64]{0,1:T(8,128)(2,1)S(1)}, u32[]{:S(2)}, u32[]{:S(2)}) collective-permute-start(bf16[256,64]{0,1:T(8,128)(2,1)S(1)} %fusion.7), channel_id=1, source_target_pairs={{0,2},{2,0},{1,3},{3,1},{4,6},{6,4},{5,7},{7,5},{8,10},{10,8},{9,1... | collective-permute-start | bytes 98312 | tf_op jit(solution)/shard_map/ppermute | solution.py:10
  12.5 3.8 %collective-permute-start.1 = (f32[32,64]{1,0:T(8,128)S(1)}, f32[32,64]{1,0:T(8,128)S(1)}, u32[]{:S(2)}, u32[]{:S(2)}) collective-permute-start(f32[32,64]{1,0:T(8,128)S(1)} %constant_dynamic-slice_fusion), channel_id=1, source_target_pairs={{0,2},{2,0},{1,3},{3,1},{4,6},{6,4},{5,7},{7,5},{8,10},{10,8},{9,1... | collective-permute-start | bytes 24584 | tf_op jit(solution)/shard_map/ppermute | solution.py:10
  16.4 5.0 %collective-permute-start.4 = (bf16[1,2048]{1,0:T(2,128)(2,1)S(1)}, bf16[1,2048]{1,0:T(2,128)(2,1)S(1)}, u32[]{:S(2)}, u32[]{:S(2)}) collective-permute-start(bf16[1,2048]{1,0:T(2,128)(2,1)S(1)} %convert_element_type.34), channel_id=1, source_target_pairs={{0,12},{4,0},{8,4},{12,8},{1,13},{5,1},{9,5},{13,9},{2,14},{6,2},{... | collective-permute-start | bytes 12296 | tf_op jit(solution)/shard_map/ppermute | solution.py:10
  20.0 4.5 %collective-permute-start.3 = (bf16[1,2048]{1,0:T(2,128)(2,1)S(1)}, bf16[1,2048]{1,0:T(2,128)(2,1)S(1)}, u32[]{:S(2)}, u32[]{:S(2)}) collective-permute-start(bf16[1,2048]{1,0:T(2,128)(2,1)S(1)} %convert_element_type.34), channel_id=1, source_target_pairs={{0,8},{4,12},{8,0},{12,4},{1,9},{5,13},{9,1},{13,5},{2,10},{6,14},... | collective-permute-start | bytes 12296 | tf_op jit(solution)/shard_map/ppermute | solution.py:10
  20.0 5.4 %collective-permute-start.2 = (bf16[1,2048]{1,0:T(2,128)(2,1)S(1)}, bf16[1,2048]{1,0:T(2,128)(2,1)S(1)}, u32[]{:S(2)}, u32[]{:S(2)}) collective-permute-start(bf16[1,2048]{1,0:T(2,128)(2,1)S(1)} %convert_element_type.34), channel_id=1, source_target_pairs={{0,4},{4,8},{8,12},{12,0},{1,5},{5,9},{9,13},{13,1},{2,6},{6,10},{... | collective-permute-start | bytes 12296 | tf_op jit(solution)/shard_map/ppermute | solution.py:10
  26.3 3.7 %collective-permute-start.5 = (f32[1,1024]{1,0:T(1,128)S(1)}, f32[1,1024]{1,0:T(1,128)S(1)}, u32[]{:S(2)}, u32[]{:S(2)}) collective-permute-start(f32[1,1024]{1,0:T(1,128)S(1)} %get-tuple-element.5), channel_id=1, source_target_pairs={{0,12},{4,0},{8,4},{12,8},{1,13},{5,1},{9,5},{13,9},{2,14},{6,2},{... | collective-permute-start | bytes 12296 | tf_op jit(solution)/shard_map/ppermute | solution.py:10
  27.0 5.4 %collective-permute-start.7 = (f32[1,1024]{1,0:T(1,128)S(1)}, f32[1,1024]{1,0:T(1,128)S(1)}, u32[]{:S(2)}, u32[]{:S(2)}) collective-permute-start(f32[1,1024]{1,0:T(1,128)S(1)} %get-tuple-element.6), channel_id=1, source_target_pairs={{0,4},{4,8},{8,12},{12,0},{1,5},{5,9},{9,13},{13,1},{2,6},{6,10},{... | collective-permute-start | bytes 12296 | tf_op jit(solution)/shard_map/ppermute | solution.py:10
  28.4 4.5 %collective-permute-start.6 = (f32[1,1024]{1,0:T(1,128)S(1)}, f32[1,1024]{1,0:T(1,128)S(1)}, u32[]{:S(2)}, u32[]{:S(2)}) collective-permute-start(f32[1,1024]{1,0:T(1,128)S(1)} %get-tuple-element.7), channel_id=1, source_target_pairs={{0,8},{4,12},{8,0},{12,4},{1,9},{5,13},{9,1},{13,5},{2,10},{6,14},... | collective-permute-start | bytes 12296 | tf_op jit(solution)/shard_map/ppermute | solution.py:10
  32.9 1.4 %collective-permute-start.10 = (f32[1,1024]{1,0:T(1,128)S(1)}, f32[1,1024]{1,0:T(1,128)S(1)}, u32[]{:S(2)}, u32[]{:S(2)}) collective-permute-start(f32[1,1024]{1,0:T(1,128)S(1)} %fusion.27), channel_id=1, source_target_pairs={{0,3},{1,0},{2,1},{3,2},{4,7},{5,4},{6,5},{7,6},{8,11},{9,8},{10,9... | collective-permute-start | bytes 12296 | tf_op jit(solution)/shard_map/ppermute | solution.py:10
  33.0 3.7 %collective-permute-start.9 = (f32[1,1024]{1,0:T(1,128)S(1)}, f32[1,1024]{1,0:T(1,128)S(1)}, u32[]{:S(2)}, u32[]{:S(2)}) collective-permute-start(f32[1,1024]{1,0:T(1,128)S(1)} %fusion.27), channel_id=1, source_target_pairs={{0,2},{1,3},{2,0},{3,1},{4,6},{5,7},{6,4},{7,5},{8,10},{9,11},{10,... | collective-permute-start | bytes 12296 | tf_op jit(solution)/shard_map/ppermute | solution.py:10
  33.6 3.1 %collective-permute-start.8 = (f32[1,1024]{1,0:T(1,128)S(1)}, f32[1,1024]{1,0:T(1,128)S(1)}, u32[]{:S(2)}, u32[]{:S(2)}) collective-permute-start(f32[1,1024]{1,0:T(1,128)S(1)} %fusion.27), channel_id=1, source_target_pairs={{0,1},{1,2},{2,3},{3,0},{4,5},{5,6},{6,7},{7,4},{8,9},{9,10},{10,1... | collective-permute-start | bytes 12296 | tf_op jit(solution)/shard_map/ppermute | solution.py:10

commit v5 on v4

--- a/solution.py
+++ b/solution.py
@@ -10,7 +10,7 @@
     return lax.ppermute(x, axis, [(i, (i + shift) % size) for i in range(size)])
 
 
-def body(hidden_in, out_grad, proj_in, proj_out, query_grads, lengths, query_decision):
+def body_inner(hidden_in, out_grad, proj_in, proj_out, query_grads, lengths, query_decision):
     tensors = lax.axis_size("tensor")
     dps = lax.axis_size("dp")
     layers = lax.axis_size("layer")
@@ -44,8 +44,10 @@
     grad_part = grad_part / length.astype(jnp.float32)
     grad_flat = grad_part.reshape(1, -1).astype(jnp.bfloat16)
 
-    grads = [grad_flat] + [shifted(grad_flat, "dp", dps, s) for s in range(1, dps)]
-    grads = jnp.concatenate(grads, axis=0)
+    got = []
+    for s in range(1, dps):
+        got.append(shifted(grad_flat, "dp", dps, s))
+    grads = jnp.concatenate([grad_flat] + got, axis=0)
     scores = jnp.dot(grads, query_rows.T, preferred_element_type=jnp.float32)
     table = (
         query_decision[:, None] == jnp.arange(DECISIONS, dtype=jnp.int32)[None, :]
@@ -76,4 +78,4 @@
         P("dp"),
     )
     out_specs = P(("groups", "dp"), None)
-    return jax.shard_map(body, mesh=mesh, in_specs=in_specs, out_specs=out_specs, check_vma=False)
+    return jax.shard_map(body_inner, mesh=mesh, in_specs=in_specs, out_specs=out_specs, check_vma=False)

time: 37.4 us -> 37.4 us (level)
  no operation moved by 1% of the time
where the time goes in v5:
time: 37.4 us; the launch traced here: 37.3 us
  waiting for transfers between devices  14.5 us (39%)
  starting transfers between devices  11.8 us (32%)
  matrix products  8.65 us (23%)
  local copies, waits for them, and re-layouts  0.91 us (2%)
  between operations  0.91 us (2%)
  other arithmetic  0.62 us (2%)
    ppermute x11, waiting for transfers between devices, shifted(): return lax.ppermute(x, axis, [(i, (i + shift) % size) for i in range(size)])  14.5 us
    ppermute x11, starting transfers between devices, shifted(): return lax.ppermute(x, axis, [(i, (i + shift) % size) for i in range(size)])  11.8 us
    dot_general x1, matrix products, body_inner(): left = jnp.dot(hidden_rows, proj_in[0], preferred_element_type=jnp.float32)  5.61 us
    dot_general x1, matrix products, body_inner(): right = jnp.dot(grad_rows, proj_out[0], preferred_element_type=jnp.float32)  1.8 us
    unnamed x6, local copies, waits for them, and re-layouts  0.8 us
  transfers between devices with their start and end apart: 11, of which 9 were waited for; matrix products, arithmetic and copies ran while one was open for 16% of the time, Pallas kernels for 0%

profile of v5, /device:TPU:0, one launch (start us, length us, event | category | flops | bytes accessed | tf_op | source)
XLA Modules:
  0.0 37.3 jit_solution(3121487364688560229)
XLA Ops:
  0.0 0.0 copy-start
  0.8 0.8 %copy-done = bf16[1,1,256,4096]{3,2,1,0:T(8,128)(2,1)S(1)} copy-done((bf16[1,1,256,4096]{3,2,1,0:T(8,128)(2,1)S(1)}, bf16[1,1,256,4096]{3,2,1,0:T(8,128)(2,1)}, u32[]{:S(2)}) %copy-start) | copy-done | bytes 2097176
  1.6 1.8 %fusion.7 = bf16[256,64]{0,1:T(8,128)(2,1)S(1)} fusion(bf16[1,1,256,4096]{3,2,1,0:T(8,128)(2,1)S(1)} %copy-done, bf16[1,4096,64]{1,2,0:T(8,128)(2,1)} %param.10, f32[256]{0:T(256)S(1)} %compare_convert_fusion), kind=kOutput, calls=%fused_computation.5 | convolution fusion | flops 134250496 | bytes 2655232 | tf_op jit(solution)/shard_map/dot_general | solution.py:26
  3.4 3.0 %collective-permute-start = (bf16[256,64]{0,1:T(8,128)(2,1)S(1)}, bf16[256,64]{0,1:T(8,128)(2,1)S(1)}, u32[]{:S(2)}, u32[]{:S(2)}) collective-permute-start(bf16[256,64]{0,1:T(8,128)(2,1)S(1)} %fusion.7), channel_id=1, source_target_pairs={{0,2},{2,0},{1,3},{3,1},{4,6},{6,4},{5,7},{7,5},{8,10},{10,8},{9,1... | collective-permute-start | bytes 98312 | tf_op jit(solution)/shard_map/ppermute | solution.py:10
  6.4 5.6 %fusion = f32[512,64]{0,1:T(8,128)S(1)} fusion(bf16[1,1,512,7168]{3,2,1,0:T(8,128)(2,1)} %param.7, bf16[1,7168,64]{1,2,0:T(8,128)(2,1)} %param.9), kind=kOutput, calls=%fused_computation | convolution fusion | flops 469762048 | bytes 8388608 | tf_op jit(solution)/shard_map/dot_general | solution.py:30
  12.0 0.2 fusion.17
  12.3 0.0 collective-permute-done
  12.3 0.2 convolution_add_fusion
  12.5 0.1 collective-permute-start.1
  12.6 3.7 %collective-permute-done.1 = f32[32,64]{1,0:T(8,128)S(1)} collective-permute-done((f32[32,64]{1,0:T(8,128)S(1)}, f32[32,64]{1,0:T(8,128)S(1)}, u32[]{:S(2)}, u32[]{:S(2)}) %collective-permute-start.1) | collective-permute-done | bytes 8224 | tf_op jit(solution)/shard_map/ppermute | solution.py:10
  16.3 0.1 convert_element_type.34
  16.4 3.6 %collective-permute-start.4 = (bf16[1,2048]{1,0:T(2,128)(2,1)S(1)}, bf16[1,2048]{1,0:T(2,128)(2,1)S(1)}, u32[]{:S(2)}, u32[]{:S(2)}) collective-permute-start(bf16[1,2048]{1,0:T(2,128)(2,1)S(1)} %convert_element_type.34), channel_id=1, source_target_pairs={{0,12},{4,0},{8,4},{12,8},{1,13},{5,1},{9,5},{13,9},{2,14},{6,2},{... | collective-permute-start | bytes 12296 | tf_op jit(solution)/shard_map/ppermute | solution.py:10
  20.0 0.0 collective-permute-start.3
  20.0 1.0 %collective-permute-start.2 = (bf16[1,2048]{1,0:T(2,128)(2,1)S(1)}, bf16[1,2048]{1,0:T(2,128)(2,1)S(1)}, u32[]{:S(2)}, u32[]{:S(2)}) collective-permute-start(bf16[1,2048]{1,0:T(2,128)(2,1)S(1)} %convert_element_type.34), channel_id=1, source_target_pairs={{0,4},{4,8},{8,12},{12,0},{1,5},{5,9},{9,13},{13,1},{2,6},{6,10},{... | collective-permute-start | bytes 12296 | tf_op jit(solution)/shard_map/ppermute | solution.py:10
  21.0 0.4 collective-permute-done.4
  21.4 3.2 %collective-permute-done.3 = bf16[1,2048]{1,0:T(2,128)(2,1)S(1)} collective-permute-done((bf16[1,2048]{1,0:T(2,128)(2,1)S(1)}, bf16[1,2048]{1,0:T(2,128)(2,1)S(1)}, u32[]{:S(2)}, u32[]{:S(2)}) %collective-permute-start.3) | collective-permute-done | bytes 4128 | tf_op jit(solution)/shard_map/ppermute | solution.py:10
  24.5 0.9 %collective-permute-done.2 = bf16[1,2048]{1,0:T(2,128)(2,1)S(1)} collective-permute-done((bf16[1,2048]{1,0:T(2,128)(2,1)S(1)}, bf16[1,2048]{1,0:T(2,128)(2,1)S(1)}, u32[]{:S(2)}, u32[]{:S(2)}) %collective-permute-start.2) | collective-permute-done | bytes 4128 | tf_op jit(solution)/shard_map/ppermute | solution.py:10
  25.4 0.4 %fusion.10 = f32[4,256]{1,0:T(4,128)S(1)} fusion(bf16[1,256,2048]{2,1,0:T(8,128)(2,1)S(1)} %copy-done.1, bf16[1,2048]{1,0:T(2,128)(2,1)S(1)} %collective-permute-done.4, bf16[1,2048]{1,0:T(2,128)(2,1)S(1)} %collective-permute-done.3, bf16[1,2048]{1,0:T(2,128)(2,1)S(1)} %collective-permute-done.2, bf16[1,2048]{1,0:T(2,128)(2,1)S(1)} %convert_element_type.34), kind=kOutput, calls=%fused_computation.7 | convolution fusion | flops 4259840 | bytes 1069056 | tf_op jit(solution)/shard_map/dot_general | solution.py:51
  25.8 0.5 %fusion.12 = f32[4,1024]{1,0:T(4,128)S(1)} fusion(f32[4,256]{1,0:T(4,128)S(1)} %fusion.10, s32[256]{0:T(256)S(1)} %copy-done.2), kind=kOutput, calls=%fused_computation.10 | convolution fusion | flops 12845056 | bytes 21504 | tf_op jit(solution)/shard_map/dot_general | solution.py:55
  26.3 0.6 %collective-permute-start.5 = (f32[1,1024]{1,0:T(1,128)S(1)}, f32[1,1024]{1,0:T(1,128)S(1)}, u32[]{:S(2)}, u32[]{:S(2)}) collective-permute-start(f32[1,1024]{1,0:T(1,128)S(1)} %get-tuple-element.5), channel_id=1, source_target_pairs={{0,12},{4,0},{8,4},{12,8},{1,13},{5,1},{9,5},{13,9},{2,14},{6,2},{... | collective-permute-start | bytes 12296 | tf_op jit(solution)/shard_map/ppermute | solution.py:10
  27.0 1.5 %collective-permute-start.7 = (f32[1,1024]{1,0:T(1,128)S(1)}, f32[1,1024]{1,0:T(1,128)S(1)}, u32[]{:S(2)}, u32[]{:S(2)}) collective-permute-start(f32[1,1024]{1,0:T(1,128)S(1)} %get-tuple-element.6), channel_id=1, source_target_pairs={{0,4},{4,8},{8,12},{12,0},{1,5},{5,9},{9,13},{13,1},{2,6},{6,10},{... | collective-permute-start | bytes 12296 | tf_op jit(solution)/shard_map/ppermute | solution.py:10
  28.4 1.1 %collective-permute-start.6 = (f32[1,1024]{1,0:T(1,128)S(1)}, f32[1,1024]{1,0:T(1,128)S(1)}, u32[]{:S(2)}, u32[]{:S(2)}) collective-permute-start(f32[1,1024]{1,0:T(1,128)S(1)} %get-tuple-element.7), channel_id=1, source_target_pairs={{0,8},{4,12},{8,0},{12,4},{1,9},{5,13},{9,1},{13,5},{2,10},{6,14},... | collective-permute-start | bytes 12296 | tf_op jit(solution)/shard_map/ppermute | solution.py:10
  29.6 0.5 %collective-permute-done.5 = f32[1,1024]{1,0:T(1,128)S(1)} collective-permute-done((f32[1,1024]{1,0:T(1,128)S(1)}, f32[1,1024]{1,0:T(1,128)S(1)}, u32[]{:S(2)}, u32[]{:S(2)}) %collective-permute-start.5) | collective-permute-done | bytes 4128 | tf_op jit(solution)/shard_map/ppermute | solution.py:10
  30.0 2.4 %collective-permute-done.7 = f32[1,1024]{1,0:T(1,128)S(1)} collective-permute-done((f32[1,1024]{1,0:T(1,128)S(1)}, f32[1,1024]{1,0:T(1,128)S(1)}, u32[]{:S(2)}, u32[]{:S(2)}) %collective-permute-start.7) | collective-permute-done | bytes 4128 | tf_op jit(solution)/shard_map/ppermute | solution.py:10
  32.4 0.6 %collective-permute-done.6 = f32[1,1024]{1,0:T(1,128)S(1)} collective-permute-done((f32[1,1024]{1,0:T(1,128)S(1)}, f32[1,1024]{1,0:T(1,128)S(1)}, u32[]{:S(2)}, u32[]{:S(2)}) %collective-permute-start.6) | collective-permute-done | bytes 4128 | tf_op jit(solution)/shard_map/ppermute | solution.py:10
  32.9 0.1 collective-permute-start.10
  33.0 0.6 %collective-permute-start.9 = (f32[1,1024]{1,0:T(1,128)S(1)}, f32[1,1024]{1,0:T(1,128)S(1)}, u32[]{:S(2)}, u32[]{:S(2)}) collective-permute-start(f32[1,1024]{1,0:T(1,128)S(1)} %fusion.27), channel_id=1, source_target_pairs={{0,2},{1,3},{2,0},{3,1},{4,6},{5,7},{6,4},{7,5},{8,10},{9,11},{10,... | collective-permute-start | bytes 12296 | tf_op jit(solution)/shard_map/ppermute | solution.py:10
  33.6 0.2 collective-permute-start.8
  33.8 0.6 %collective-permute-done.10 = f32[1,1024]{1,0:T(1,128)S(1)} collective-permute-done((f32[1,1024]{1,0:T(1,128)S(1)}, f32[1,1024]{1,0:T(1,128)S(1)}, u32[]{:S(2)}, u32[]{:S(2)}) %collective-permute-start.10) | collective-permute-done | bytes 4128 | tf_op jit(solution)/shard_map/ppermute | solution.py:10
  34.3 2.4 %collective-permute-done.9 = f32[1,1024]{1,0:T(1,128)S(1)} collective-permute-done((f32[1,1024]{1,0:T(1,128)S(1)}, f32[1,1024]{1,0:T(1,128)S(1)}, u32[]{:S(2)}, u32[]{:S(2)}) %collective-permute-start.9) | collective-permute-done | bytes 4128 | tf_op jit(solution)/shard_map/ppermute | solution.py:10
  36.7 0.0 collective-permute-done.8
  36.7 0.6 %add_add_fusion = f32[1,1024]{1,0:T(1,128)} fusion(f32[1,1024]{1,0:T(1,128)S(1)} %fusion.27, f32[1,1024]{1,0:T(1,128)S(1)} %collective-permute-done.10, f32[1,1024]{1,0:T(1,128)S(1)} %collective-permute-done.8, f32[1,1024]{1,0:T(1,128)S(1)} %collective-permute-done.9), kind=kLoop, calls=%fused_computation.28 | loop fusion | flops 3072 | bytes 20480 | tf_op jit(solution)/shard_map/add | solution.py:64
  (9 shorter events, 0.1 us)
Async XLA Ops:
  0.0 1.6 %copy-start = (bf16[1,1,256,4096]{3,2,1,0:T(8,128)(2,1)S(1)}, bf16[1,1,256,4096]{3,2,1,0:T(8,128)(2,1)}, u32[]{:S(2)}) copy-start(bf16[1,1,256,4096]{3,2,1,0:T(8,128)(2,1)} %param.8) | copy-start | bytes 6291460
  0.0 25.4 %copy-start.1 = (bf16[1,256,2048]{2,1,0:T(8,128)(2,1)S(1)}, bf16[1,256,2048]{2,1,0:T(8,128)(2,1)}, u32[]{:S(2)}) copy-start(bf16[1,256,2048]{2,1,0:T(8,128)(2,1)} %param.11) | copy-start | bytes 3145732
  0.0 25.8 %copy-start.2 = (s32[256]{0:T(256)S(1)}, s32[256]{0:T(256)}, u32[]{:S(2)}) copy-start(s32[256]{0:T(256)} %param.13) | copy-start | bytes 3076
  3.4 8.9 %collective-permute-start = (bf16[256,64]{0,1:T(8,128)(2,1)S(1)}, bf16[256,64]{0,1:T(8,128)(2,1)S(1)}, u32[]{:S(2)}, u32[]{:S(2)}) collective-permute-start(bf16[256,64]{0,1:T(8,128)(2,1)S(1)} %fusion.7), channel_id=1, source_target_pairs={{0,2},{2,0},{1,3},{3,1},{4,6},{6,4},{5,7},{7,5},{8,10},{10,8},{9,1... | collective-permute-start | bytes 98312 | tf_op jit(solution)/shard_map/ppermute | solution.py:10
  12.5 3.8 %collective-permute-start.1 = (f32[32,64]{1,0:T(8,128)S(1)}, f32[32,64]{1,0:T(8,128)S(1)}, u32[]{:S(2)}, u32[]{:S(2)}) collective-permute-start(f32[32,64]{1,0:T(8,128)S(1)} %constant_dynamic-slice_fusion), channel_id=1, source_target_pairs={{0,2},{2,0},{1,3},{3,1},{4,6},{6,4},{5,7},{7,5},{8,10},{10,8},{9,1... | collective-permute-start | bytes 24584 | tf_op jit(solution)/shard_map/ppermute | solution.py:10
  16.4 5.0 %collective-permute-start.4 = (bf16[1,2048]{1,0:T(2,128)(2,1)S(1)}, bf16[1,2048]{1,0:T(2,128)(2,1)S(1)}, u32[]{:S(2)}, u32[]{:S(2)}) collective-permute-start(bf16[1,2048]{1,0:T(2,128)(2,1)S(1)} %convert_element_type.34), channel_id=1, source_target_pairs={{0,12},{4,0},{8,4},{12,8},{1,13},{5,1},{9,5},{13,9},{2,14},{6,2},{... | collective-permute-start | bytes 12296 | tf_op jit(solution)/shard_map/ppermute | solution.py:10
  20.0 4.5 %collective-permute-start.3 = (bf16[1,2048]{1,0:T(2,128)(2,1)S(1)}, bf16[1,2048]{1,0:T(2,128)(2,1)S(1)}, u32[]{:S(2)}, u32[]{:S(2)}) collective-permute-start(bf16[1,2048]{1,0:T(2,128)(2,1)S(1)} %convert_element_type.34), channel_id=1, source_target_pairs={{0,8},{4,12},{8,0},{12,4},{1,9},{5,13},{9,1},{13,5},{2,10},{6,14},... | collective-permute-start | bytes 12296 | tf_op jit(solution)/shard_map/ppermute | solution.py:10
  20.0 5.4 %collective-permute-start.2 = (bf16[1,2048]{1,0:T(2,128)(2,1)S(1)}, bf16[1,2048]{1,0:T(2,128)(2,1)S(1)}, u32[]{:S(2)}, u32[]{:S(2)}) collective-permute-start(bf16[1,2048]{1,0:T(2,128)(2,1)S(1)} %convert_element_type.34), channel_id=1, source_target_pairs={{0,4},{4,8},{8,12},{12,0},{1,5},{5,9},{9,13},{13,1},{2,6},{6,10},{... | collective-permute-start | bytes 12296 | tf_op jit(solution)/shard_map/ppermute | solution.py:10
  26.3 3.7 %collective-permute-start.5 = (f32[1,1024]{1,0:T(1,128)S(1)}, f32[1,1024]{1,0:T(1,128)S(1)}, u32[]{:S(2)}, u32[]{:S(2)}) collective-permute-start(f32[1,1024]{1,0:T(1,128)S(1)} %get-tuple-element.5), channel_id=1, source_target_pairs={{0,12},{4,0},{8,4},{12,8},{1,13},{5,1},{9,5},{13,9},{2,14},{6,2},{... | collective-permute-start | bytes 12296 | tf_op jit(solution)/shard_map/ppermute | solution.py:10
  27.0 5.4 %collective-permute-start.7 = (f32[1,1024]{1,0:T(1,128)S(1)}, f32[1,1024]{1,0:T(1,128)S(1)}, u32[]{:S(2)}, u32[]{:S(2)}) collective-permute-start(f32[1,1024]{1,0:T(1,128)S(1)} %get-tuple-element.6), channel_id=1, source_target_pairs={{0,4},{4,8},{8,12},{12,0},{1,5},{5,9},{9,13},{13,1},{2,6},{6,10},{... | collective-permute-start | bytes 12296 | tf_op jit(solution)/shard_map/ppermute | solution.py:10
  28.4 4.5 %collective-permute-start.6 = (f32[1,1024]{1,0:T(1,128)S(1)}, f32[1,1024]{1,0:T(1,128)S(1)}, u32[]{:S(2)}, u32[]{:S(2)}) collective-permute-start(f32[1,1024]{1,0:T(1,128)S(1)} %get-tuple-element.7), channel_id=1, source_target_pairs={{0,8},{4,12},{8,0},{12,4},{1,9},{5,13},{9,1},{13,5},{2,10},{6,14},... | collective-permute-start | bytes 12296 | tf_op jit(solution)/shard_map/ppermute | solution.py:10
  32.9 1.4 %collective-permute-start.10 = (f32[1,1024]{1,0:T(1,128)S(1)}, f32[1,1024]{1,0:T(1,128)S(1)}, u32[]{:S(2)}, u32[]{:S(2)}) collective-permute-start(f32[1,1024]{1,0:T(1,128)S(1)} %fusion.27), channel_id=1, source_target_pairs={{0,3},{1,0},{2,1},{3,2},{4,7},{5,4},{6,5},{7,6},{8,11},{9,8},{10,9... | collective-permute-start | bytes 12296 | tf_op jit(solution)/shard_map/ppermute | solution.py:10
  33.0 3.7 %collective-permute-start.9 = (f32[1,1024]{1,0:T(1,128)S(1)}, f32[1,1024]{1,0:T(1,128)S(1)}, u32[]{:S(2)}, u32[]{:S(2)}) collective-permute-start(f32[1,1024]{1,0:T(1,128)S(1)} %fusion.27), channel_id=1, source_target_pairs={{0,2},{1,3},{2,0},{3,1},{4,6},{5,7},{6,4},{7,5},{8,10},{9,11},{10,... | collective-permute-start | bytes 12296 | tf_op jit(solution)/shard_map/ppermute | solution.py:10
  33.6 3.1 %collective-permute-start.8 = (f32[1,1024]{1,0:T(1,128)S(1)}, f32[1,1024]{1,0:T(1,128)S(1)}, u32[]{:S(2)}, u32[]{:S(2)}) collective-permute-start(f32[1,1024]{1,0:T(1,128)S(1)} %fusion.27), channel_id=1, source_target_pairs={{0,1},{1,2},{2,3},{3,0},{4,5},{5,6},{6,7},{7,4},{8,9},{9,10},{10,1... | collective-permute-start | bytes 12296 | tf_op jit(solution)/shard_map/ppermute | solution.py:10

commit v6 on v5

--- a/solution.py
+++ b/solution.py
@@ -59,10 +59,15 @@
         total = total + shifted(partial_dec[s : s + 1], "dp", dps, -s)
 
     peers = tensors * layers
-    if peers <= 4:
-        gathered = [shifted(total, ("tensor", "layer"), peers, s) for s in range(1, peers)]
-        total = total + sum(gathered)
-    else:
+    if peers in (2, 4):
+        flip = [
+            lax.ppermute(total, ("tensor", "layer"), [(i, i ^ m) for i in range(peers)])
+            for m in range(1, peers)
+        ]
+        total = total + flip[0]
+        if peers == 4:
+            total = total + (flip[1] + flip[2])
+    elif peers > 1:
         total = lax.psum(total, ("tensor", "layer"))
     return total
 

time: 37.4 us -> 37.5 us (level)
  starting transfers between devices: 11.8 us -> 12.9 us
  waiting for transfers between devices: 14.5 us -> 13.4 us
    ppermute x11 -> x8, waiting for transfers between devices: 14.5 us -> 11.5 us  [shifted(): return lax.ppermute(x, axis, [(i, (i + shift) % size) for i in range(size)])]
    ppermute x0 -> x3, starting transfers between devices: none -> 1.92 us  [body_inner(): lax.ppermute(total, ('tensor', 'layer'), [(i, i ^ m) for i in range(peers)])]
    ppermute x0 -> x3, waiting for transfers between devices: none -> 1.83 us  [body_inner(): lax.ppermute(total, ('tensor', 'layer'), [(i, i ^ m) for i in range(peers)])]
    ppermute x11 -> x8, starting transfers between devices: 11.8 us -> 10.9 us  [shifted(): return lax.ppermute(x, axis, [(i, (i + shift) % size) for i in range(size)])]
where the time goes in v6:
time: 37.5 us; the launch traced here: 37.3 us
  waiting for transfers between devices  13.4 us (36%)
  starting transfers between devices  12.9 us (34%)
  matrix products  8.65 us (23%)
  local copies, waits for them, and re-layouts  0.91 us (2%)
  between operations  0.91 us (2%)
  other arithmetic  0.62 us (2%)
    ppermute x8, waiting for transfers between devices, shifted(): return lax.ppermute(x, axis, [(i, (i + shift) % size) for i in range(size)])  11.5 us
    ppermute x8, starting transfers between devices, shifted(): return lax.ppermute(x, axis, [(i, (i + shift) % size) for i in range(size)])  10.9 us
    dot_general x1, matrix products, body_inner(): left = jnp.dot(hidden_rows, proj_in[0], preferred_element_type=jnp.float32)  5.61 us
    ppermute x3, starting transfers between devices, body_inner(): lax.ppermute(total, ('tensor', 'layer'), [(i, i ^ m) for i in range(peers)])  1.92 us
    ppermute x3, waiting for transfers between devices, body_inner(): lax.ppermute(total, ('tensor', 'layer'), [(i, i ^ m) for i in range(peers)])  1.83 us
    dot_general x1, matrix products, body_inner(): right = jnp.dot(grad_rows, proj_out[0], preferred_element_type=jnp.float32)  1.8 us
    unnamed x6, local copies, waits for them, and re-layouts  0.8 us
  transfers between devices with their start and end apart: 11, of which 9 were waited for; matrix products, arithmetic and copies ran while one was open for 16% of the time, Pallas kernels for 0%

profile of v6, /device:TPU:0, one launch (start us, length us, event | category | flops | bytes accessed | tf_op | source)
XLA Modules:
  0.0 37.3 jit_solution(2136283793489423448)
XLA Ops:
  0.0 0.0 copy-start
  0.8 0.8 %copy-done = bf16[1,1,256,4096]{3,2,1,0:T(8,128)(2,1)S(1)} copy-done((bf16[1,1,256,4096]{3,2,1,0:T(8,128)(2,1)S(1)}, bf16[1,1,256,4096]{3,2,1,0:T(8,128)(2,1)}, u32[]{:S(2)}) %copy-start) | copy-done | bytes 2097176
  1.6 1.8 %fusion.7 = bf16[256,64]{0,1:T(8,128)(2,1)S(1)} fusion(bf16[1,1,256,4096]{3,2,1,0:T(8,128)(2,1)S(1)} %copy-done, bf16[1,4096,64]{1,2,0:T(8,128)(2,1)} %param.10, f32[256]{0:T(256)S(1)} %compare_convert_fusion), kind=kOutput, calls=%fused_computation.5 | convolution fusion | flops 134250496 | bytes 2655232 | tf_op jit(solution)/shard_map/dot_general | solution.py:26
  3.4 3.0 %collective-permute-start = (bf16[256,64]{0,1:T(8,128)(2,1)S(1)}, bf16[256,64]{0,1:T(8,128)(2,1)S(1)}, u32[]{:S(2)}, u32[]{:S(2)}) collective-permute-start(bf16[256,64]{0,1:T(8,128)(2,1)S(1)} %fusion.7), channel_id=1, source_target_pairs={{0,2},{2,0},{1,3},{3,1},{4,6},{6,4},{5,7},{7,5},{8,10},{10,8},{9,1... | collective-permute-start | bytes 98312 | tf_op jit(solution)/shard_map/ppermute | solution.py:10
  6.4 5.6 %fusion = f32[512,64]{0,1:T(8,128)S(1)} fusion(bf16[1,1,512,7168]{3,2,1,0:T(8,128)(2,1)} %param.7, bf16[1,7168,64]{1,2,0:T(8,128)(2,1)} %param.9), kind=kOutput, calls=%fused_computation | convolution fusion | flops 469762048 | bytes 8388608 | tf_op jit(solution)/shard_map/dot_general | solution.py:30
  12.0 0.2 fusion.17
  12.3 0.0 collective-permute-done
  12.3 0.2 convolution_add_fusion
  12.5 0.1 collective-permute-start.1
  12.6 3.7 %collective-permute-done.1 = f32[32,64]{1,0:T(8,128)S(1)} collective-permute-done((f32[32,64]{1,0:T(8,128)S(1)}, f32[32,64]{1,0:T(8,128)S(1)}, u32[]{:S(2)}, u32[]{:S(2)}) %collective-permute-start.1) | collective-permute-done | bytes 8224 | tf_op jit(solution)/shard_map/ppermute | solution.py:10
  16.3 0.1 convert_element_type.34
  16.4 3.6 %collective-permute-start.4 = (bf16[1,2048]{1,0:T(2,128)(2,1)S(1)}, bf16[1,2048]{1,0:T(2,128)(2,1)S(1)}, u32[]{:S(2)}, u32[]{:S(2)}) collective-permute-start(bf16[1,2048]{1,0:T(2,128)(2,1)S(1)} %convert_element_type.34), channel_id=1, source_target_pairs={{0,12},{4,0},{8,4},{12,8},{1,13},{5,1},{9,5},{13,9},{2,14},{6,2},{... | collective-permute-start | bytes 12296 | tf_op jit(solution)/shard_map/ppermute | solution.py:10
  20.0 0.0 collective-permute-start.3
  20.0 1.0 %collective-permute-start.2 = (bf16[1,2048]{1,0:T(2,128)(2,1)S(1)}, bf16[1,2048]{1,0:T(2,128)(2,1)S(1)}, u32[]{:S(2)}, u32[]{:S(2)}) collective-permute-start(bf16[1,2048]{1,0:T(2,128)(2,1)S(1)} %convert_element_type.34), channel_id=1, source_target_pairs={{0,4},{4,8},{8,12},{12,0},{1,5},{5,9},{9,13},{13,1},{2,6},{6,10},{... | collective-permute-start | bytes 12296 | tf_op jit(solution)/shard_map/ppermute | solution.py:10
  21.0 0.4 collective-permute-done.4
  21.4 3.2 %collective-permute-done.3 = bf16[1,2048]{1,0:T(2,128)(2,1)S(1)} collective-permute-done((bf16[1,2048]{1,0:T(2,128)(2,1)S(1)}, bf16[1,2048]{1,0:T(2,128)(2,1)S(1)}, u32[]{:S(2)}, u32[]{:S(2)}) %collective-permute-start.3) | collective-permute-done | bytes 4128 | tf_op jit(solution)/shard_map/ppermute | solution.py:10
  24.5 0.9 %collective-permute-done.2 = bf16[1,2048]{1,0:T(2,128)(2,1)S(1)} collective-permute-done((bf16[1,2048]{1,0:T(2,128)(2,1)S(1)}, bf16[1,2048]{1,0:T(2,128)(2,1)S(1)}, u32[]{:S(2)}, u32[]{:S(2)}) %collective-permute-start.2) | collective-permute-done | bytes 4128 | tf_op jit(solution)/shard_map/ppermute | solution.py:10
  25.4 0.4 %fusion.10 = f32[4,256]{1,0:T(4,128)S(1)} fusion(bf16[1,256,2048]{2,1,0:T(8,128)(2,1)S(1)} %copy-done.1, bf16[1,2048]{1,0:T(2,128)(2,1)S(1)} %collective-permute-done.4, bf16[1,2048]{1,0:T(2,128)(2,1)S(1)} %collective-permute-done.3, bf16[1,2048]{1,0:T(2,128)(2,1)S(1)} %collective-permute-done.2, bf16[1,2048]{1,0:T(2,128)(2,1)S(1)} %convert_element_type.34), kind=kOutput, calls=%fused_computation.7 | convolution fusion | flops 4259840 | bytes 1069056 | tf_op jit(solution)/shard_map/dot_general | solution.py:51
  25.8 0.5 %fusion.12 = f32[4,1024]{1,0:T(4,128)S(1)} fusion(f32[4,256]{1,0:T(4,128)S(1)} %fusion.10, s32[256]{0:T(256)S(1)} %copy-done.2), kind=kOutput, calls=%fused_computation.10 | convolution fusion | flops 12845056 | bytes 21504 | tf_op jit(solution)/shard_map/dot_general | solution.py:55
  26.3 0.6 %collective-permute-start.5 = (f32[1,1024]{1,0:T(1,128)S(1)}, f32[1,1024]{1,0:T(1,128)S(1)}, u32[]{:S(2)}, u32[]{:S(2)}) collective-permute-start(f32[1,1024]{1,0:T(1,128)S(1)} %get-tuple-element.5), channel_id=1, source_target_pairs={{0,12},{4,0},{8,4},{12,8},{1,13},{5,1},{9,5},{13,9},{2,14},{6,2},{... | collective-permute-start | bytes 12296 | tf_op jit(solution)/shard_map/ppermute | solution.py:10
  27.0 1.5 %collective-permute-start.7 = (f32[1,1024]{1,0:T(1,128)S(1)}, f32[1,1024]{1,0:T(1,128)S(1)}, u32[]{:S(2)}, u32[]{:S(2)}) collective-permute-start(f32[1,1024]{1,0:T(1,128)S(1)} %get-tuple-element.6), channel_id=1, source_target_pairs={{0,4},{4,8},{8,12},{12,0},{1,5},{5,9},{9,13},{13,1},{2,6},{6,10},{... | collective-permute-start | bytes 12296 | tf_op jit(solution)/shard_map/ppermute | solution.py:10
  28.4 1.1 %collective-permute-start.6 = (f32[1,1024]{1,0:T(1,128)S(1)}, f32[1,1024]{1,0:T(1,128)S(1)}, u32[]{:S(2)}, u32[]{:S(2)}) collective-permute-start(f32[1,1024]{1,0:T(1,128)S(1)} %get-tuple-element.7), channel_id=1, source_target_pairs={{0,8},{4,12},{8,0},{12,4},{1,9},{5,13},{9,1},{13,5},{2,10},{6,14},... | collective-permute-start | bytes 12296 | tf_op jit(solution)/shard_map/ppermute | solution.py:10
  29.6 0.5 %collective-permute-done.5 = f32[1,1024]{1,0:T(1,128)S(1)} collective-permute-done((f32[1,1024]{1,0:T(1,128)S(1)}, f32[1,1024]{1,0:T(1,128)S(1)}, u32[]{:S(2)}, u32[]{:S(2)}) %collective-permute-start.5) | collective-permute-done | bytes 4128 | tf_op jit(solution)/shard_map/ppermute | solution.py:10
  30.0 2.4 %collective-permute-done.7 = f32[1,1024]{1,0:T(1,128)S(1)} collective-permute-done((f32[1,1024]{1,0:T(1,128)S(1)}, f32[1,1024]{1,0:T(1,128)S(1)}, u32[]{:S(2)}, u32[]{:S(2)}) %collective-permute-start.7) | collective-permute-done | bytes 4128 | tf_op jit(solution)/shard_map/ppermute | solution.py:10
  32.4 0.6 %collective-permute-done.6 = f32[1,1024]{1,0:T(1,128)S(1)} collective-permute-done((f32[1,1024]{1,0:T(1,128)S(1)}, f32[1,1024]{1,0:T(1,128)S(1)}, u32[]{:S(2)}, u32[]{:S(2)}) %collective-permute-start.6) | collective-permute-done | bytes 4128 | tf_op jit(solution)/shard_map/ppermute | solution.py:10
  32.9 0.1 collective-permute-start.10
  33.0 0.6 %collective-permute-start.9 = (f32[1,1024]{1,0:T(1,128)S(1)}, f32[1,1024]{1,0:T(1,128)S(1)}, u32[]{:S(2)}, u32[]{:S(2)}) collective-permute-start(f32[1,1024]{1,0:T(1,128)S(1)} %fusion.27), channel_id=1, source_target_pairs={{0,2},{1,3},{2,0},{3,1},{4,6},{5,7},{6,4},{7,5},{8,10},{9,11},{10,... | collective-permute-start | bytes 12296 | tf_op jit(solution)/shard_map/ppermute | solution.py:64
  33.6 1.2 %collective-permute-start.8 = (f32[1,1024]{1,0:T(1,128)S(1)}, f32[1,1024]{1,0:T(1,128)S(1)}, u32[]{:S(2)}, u32[]{:S(2)}) collective-permute-start(f32[1,1024]{1,0:T(1,128)S(1)} %fusion.27), channel_id=1, source_target_pairs={{0,1},{1,0},{2,3},{3,2},{4,5},{5,4},{6,7},{7,6},{8,9},{9,8},{10,11... | collective-permute-start | bytes 12296 | tf_op jit(solution)/shard_map/ppermute | solution.py:64
  34.9 1.2 %collective-permute-done.10 = f32[1,1024]{1,0:T(1,128)S(1)} collective-permute-done((f32[1,1024]{1,0:T(1,128)S(1)}, f32[1,1024]{1,0:T(1,128)S(1)}, u32[]{:S(2)}, u32[]{:S(2)}) %collective-permute-start.10) | collective-permute-done | bytes 4128 | tf_op jit(solution)/shard_map/ppermute | solution.py:64
  36.0 0.7 %collective-permute-done.9 = f32[1,1024]{1,0:T(1,128)S(1)} collective-permute-done((f32[1,1024]{1,0:T(1,128)S(1)}, f32[1,1024]{1,0:T(1,128)S(1)}, u32[]{:S(2)}, u32[]{:S(2)}) %collective-permute-start.9) | collective-permute-done | bytes 4128 | tf_op jit(solution)/shard_map/ppermute | solution.py:64
  36.7 0.0 collective-permute-done.8
  36.7 0.6 %add_add_fusion = f32[1,1024]{1,0:T(1,128)} fusion(f32[1,1024]{1,0:T(1,128)S(1)} %collective-permute-done.9, f32[1,1024]{1,0:T(1,128)S(1)} %collective-permute-done.10, f32[1,1024]{1,0:T(1,128)S(1)} %fusion.27, f32[1,1024]{1,0:T(1,128)S(1)} %collective-permute-done.8), kind=kLoop, calls=%fused_computation.28 | loop fusion | flops 3072 | bytes 20480 | tf_op jit(solution)/shard_map/add | solution.py:69
  (9 shorter events, 0.1 us)
Async XLA Ops:
  0.0 1.6 %copy-start = (bf16[1,1,256,4096]{3,2,1,0:T(8,128)(2,1)S(1)}, bf16[1,1,256,4096]{3,2,1,0:T(8,128)(2,1)}, u32[]{:S(2)}) copy-start(bf16[1,1,256,4096]{3,2,1,0:T(8,128)(2,1)} %param.8) | copy-start | bytes 6291460
  0.0 25.4 %copy-start.1 = (bf16[1,256,2048]{2,1,0:T(8,128)(2,1)S(1)}, bf16[1,256,2048]{2,1,0:T(8,128)(2,1)}, u32[]{:S(2)}) copy-start(bf16[1,256,2048]{2,1,0:T(8,128)(2,1)} %param.11) | copy-start | bytes 3145732
  0.0 25.8 %copy-start.2 = (s32[256]{0:T(256)S(1)}, s32[256]{0:T(256)}, u32[]{:S(2)}) copy-start(s32[256]{0:T(256)} %param.13) | copy-start | bytes 3076
  3.4 8.9 %collective-permute-start = (bf16[256,64]{0,1:T(8,128)(2,1)S(1)}, bf16[256,64]{0,1:T(8,128)(2,1)S(1)}, u32[]{:S(2)}, u32[]{:S(2)}) collective-permute-start(bf16[256,64]{0,1:T(8,128)(2,1)S(1)} %fusion.7), channel_id=1, source_target_pairs={{0,2},{2,0},{1,3},{3,1},{4,6},{6,4},{5,7},{7,5},{8,10},{10,8},{9,1... | collective-permute-start | bytes 98312 | tf_op jit(solution)/shard_map/ppermute | solution.py:10
  12.5 3.8 %collective-permute-start.1 = (f32[32,64]{1,0:T(8,128)S(1)}, f32[32,64]{1,0:T(8,128)S(1)}, u32[]{:S(2)}, u32[]{:S(2)}) collective-permute-start(f32[32,64]{1,0:T(8,128)S(1)} %constant_dynamic-slice_fusion), channel_id=1, source_target_pairs={{0,2},{2,0},{1,3},{3,1},{4,6},{6,4},{5,7},{7,5},{8,10},{10,8},{9,1... | collective-permute-start | bytes 24584 | tf_op jit(solution)/shard_map/ppermute | solution.py:10
  16.4 5.0 %collective-permute-start.4 = (bf16[1,2048]{1,0:T(2,128)(2,1)S(1)}, bf16[1,2048]{1,0:T(2,128)(2,1)S(1)}, u32[]{:S(2)}, u32[]{:S(2)}) collective-permute-start(bf16[1,2048]{1,0:T(2,128)(2,1)S(1)} %convert_element_type.34), channel_id=1, source_target_pairs={{0,12},{4,0},{8,4},{12,8},{1,13},{5,1},{9,5},{13,9},{2,14},{6,2},{... | collective-permute-start | bytes 12296 | tf_op jit(solution)/shard_map/ppermute | solution.py:10
  20.0 4.5 %collective-permute-start.3 = (bf16[1,2048]{1,0:T(2,128)(2,1)S(1)}, bf16[1,2048]{1,0:T(2,128)(2,1)S(1)}, u32[]{:S(2)}, u32[]{:S(2)}) collective-permute-start(bf16[1,2048]{1,0:T(2,128)(2,1)S(1)} %convert_element_type.34), channel_id=1, source_target_pairs={{0,8},{4,12},{8,0},{12,4},{1,9},{5,13},{9,1},{13,5},{2,10},{6,14},... | collective-permute-start | bytes 12296 | tf_op jit(solution)/shard_map/ppermute | solution.py:10
  20.0 5.4 %collective-permute-start.2 = (bf16[1,2048]{1,0:T(2,128)(2,1)S(1)}, bf16[1,2048]{1,0:T(2,128)(2,1)S(1)}, u32[]{:S(2)}, u32[]{:S(2)}) collective-permute-start(bf16[1,2048]{1,0:T(2,128)(2,1)S(1)} %convert_element_type.34), channel_id=1, source_target_pairs={{0,4},{4,8},{8,12},{12,0},{1,5},{5,9},{9,13},{13,1},{2,6},{6,10},{... | collective-permute-start | bytes 12296 | tf_op jit(solution)/shard_map/ppermute | solution.py:10
  26.3 3.7 %collective-permute-start.5 = (f32[1,1024]{1,0:T(1,128)S(1)}, f32[1,1024]{1,0:T(1,128)S(1)}, u32[]{:S(2)}, u32[]{:S(2)}) collective-permute-start(f32[1,1024]{1,0:T(1,128)S(1)} %get-tuple-element.5), channel_id=1, source_target_pairs={{0,12},{4,0},{8,4},{12,8},{1,13},{5,1},{9,5},{13,9},{2,14},{6,2},{... | collective-permute-start | bytes 12296 | tf_op jit(solution)/shard_map/ppermute | solution.py:10
  27.0 5.4 %collective-permute-start.7 = (f32[1,1024]{1,0:T(1,128)S(1)}, f32[1,1024]{1,0:T(1,128)S(1)}, u32[]{:S(2)}, u32[]{:S(2)}) collective-permute-start(f32[1,1024]{1,0:T(1,128)S(1)} %get-tuple-element.6), channel_id=1, source_target_pairs={{0,4},{4,8},{8,12},{12,0},{1,5},{5,9},{9,13},{13,1},{2,6},{6,10},{... | collective-permute-start | bytes 12296 | tf_op jit(solution)/shard_map/ppermute | solution.py:10
  28.4 4.5 %collective-permute-start.6 = (f32[1,1024]{1,0:T(1,128)S(1)}, f32[1,1024]{1,0:T(1,128)S(1)}, u32[]{:S(2)}, u32[]{:S(2)}) collective-permute-start(f32[1,1024]{1,0:T(1,128)S(1)} %get-tuple-element.7), channel_id=1, source_target_pairs={{0,8},{4,12},{8,0},{12,4},{1,9},{5,13},{9,1},{13,5},{2,10},{6,14},... | collective-permute-start | bytes 12296 | tf_op jit(solution)/shard_map/ppermute | solution.py:10
  32.9 3.1 %collective-permute-start.10 = (f32[1,1024]{1,0:T(1,128)S(1)}, f32[1,1024]{1,0:T(1,128)S(1)}, u32[]{:S(2)}, u32[]{:S(2)}) collective-permute-start(f32[1,1024]{1,0:T(1,128)S(1)} %fusion.27), channel_id=1, source_target_pairs={{0,3},{1,2},{2,1},{3,0},{4,7},{5,6},{6,5},{7,4},{8,11},{9,10},{10,... | collective-permute-start | bytes 12296 | tf_op jit(solution)/shard_map/ppermute | solution.py:64
  33.0 3.7 %collective-permute-start.9 = (f32[1,1024]{1,0:T(1,128)S(1)}, f32[1,1024]{1,0:T(1,128)S(1)}, u32[]{:S(2)}, u32[]{:S(2)}) collective-permute-start(f32[1,1024]{1,0:T(1,128)S(1)} %fusion.27), channel_id=1, source_target_pairs={{0,2},{1,3},{2,0},{3,1},{4,6},{5,7},{6,4},{7,5},{8,10},{9,11},{10,... | collective-permute-start | bytes 12296 | tf_op jit(solution)/shard_map/ppermute | solution.py:64
  33.6 3.1 %collective-permute-start.8 = (f32[1,1024]{1,0:T(1,128)S(1)}, f32[1,1024]{1,0:T(1,128)S(1)}, u32[]{:S(2)}, u32[]{:S(2)}) collective-permute-start(f32[1,1024]{1,0:T(1,128)S(1)} %fusion.27), channel_id=1, source_target_pairs={{0,1},{1,0},{2,3},{3,2},{4,5},{5,4},{6,7},{7,6},{8,9},{9,8},{10,11... | collective-permute-start | bytes 12296 | tf_op jit(solution)/shard_map/ppermute | solution.py:64
